TPU v7x, 128 devices: a whole 4x4x4 slice. The times are simulated.
128 devices in a mesh: tok: 16 (over z, y), head: 8 (over x, core).
Axes of the slice: x: 4, y: 4, z: 4, core: 2. Of those that a mesh axis runs over, the one named last changes fastest.
Arguments:
- hidden_in: bfloat16 [16384, 2048], P(('tok', 'head')), may hold values from -6 to 6
- context_len: int32 [16], P('tok'), may hold values from 1 to 2048, 16384 in all
- page_table: int32 [16, 16], P('tok'), may hold values from 0 to 15, as said below
- paged_cache: bfloat16 [2, 256, 128, 2048], P(None, 'tok', None, 'head'), may hold values from -139 to 139
- attn_gain: bfloat16 [2048], replicated, may hold values from 0.5 to 1.5
- proj_weight: bfloat16 [3, 2048, 2048], P(None, None, 'head'), may hold values from -0.125 to 0.125
- proj_bias: bfloat16 [3, 2048], P(None, 'head'), may hold values from -3 to 3
- out_weight: bfloat16 [2048, 2048], P('head'), may hold values from -0.125 to 0.125
- mlp_gain: bfloat16 [2048], replicated, may hold values from 0.5 to 1.5
- expert_ids: int32 [16384, 4], P(('tok', 'head')), may hold values from 0 to 63, all different within a row; in each aligned block of 128 rows (0 to 127, 128 to 255, ...) at most 10 rows name the same one
- route_weight: float32 [16384, 4], P(('tok', 'head')), may hold values from 0.05 to 0.5
- w_experts_in: bfloat16 [128, 2048, 1408], P(('tok', 'head')), may hold values from -0.125 to 0.125
- w_experts_out: bfloat16 [128, 704, 2048], P(('tok', 'head')), may hold values from -0.15625 to 0.15625
- w_shared_in: bfloat16 [2048, 2, 5632], P(None, None, 'head'), may hold values from -0.125 to 0.125
- w_shared_out: bfloat16 [5632, 2048], P('head'), may hold values from -0.078125 to 0.078125
- shared_gate: bfloat16 [2048], replicated, may hold values from -0.125 to 0.125
Outputs:
- layer_out: bfloat16 [16384, 2048], P(('tok', 'head'))
Inputs may be any that keep to these rules, and one draw needn't show every extreme that they name: `page_table`: each row is a permutation of the pool's pages. `context_len`: some request has exactly 2048 cached tokens. `expert_ids`: the experts of a row differ; within the 128 rows of one device no expert is named more than 10 times, a bound that some block reaches.
All inputs are finite; a program needn't handle non-finite values. No bound on the sum of `context_len` on one device may be relied on, other than what follows from the above.
Results may differ from a plain program's by a relative error of at most 0.02.
Values may be sent and summed in bfloat16 or wider, within the bound.
No kernel may reach another device: no remote copies, remote signals or barrier semaphores. Data moves between devices by JAX's collectives and lax.ppermute only.
A program may use at most 128 MiB of HBM per device.

v0:
```python
import math

import jax
import jax.numpy as jnp
from jax import lax
from jax.experimental import pallas as pl
from jax.experimental.pallas import tpu as pltpu
from jax.sharding import Mesh, PartitionSpec as P

HD = 128
HEAD = ("x", "core")
ROWS = ("tok", "x", "core")


EPS = 1e-06
THETA = 1000000.0


def rms_scale(values, gain):
    wide = values.astype(jnp.float32)
    spread = jnp.mean(wide * wide, axis=-1, keepdims=True)
    return (wide * lax.rsqrt(spread + EPS) * gain.astype(jnp.float32)).astype(jnp.bfloat16)


def rotate(vectors, positions):
    middle = vectors.shape[-1] // 2
    frequency = THETA ** (-(jnp.arange(middle, dtype=jnp.float32) * 2.0 / vectors.shape[-1]))
    angles = positions.astype(jnp.float32)[:, None] * frequency[None, :]
    angles = jnp.concatenate([angles, angles], axis=-1)[:, None, :]
    turned = jnp.concatenate([-vectors[..., middle:], vectors[..., :middle]], axis=-1)
    return vectors * jnp.cos(angles) + turned * jnp.sin(angles)


def attend(queries, keys_all, values_all, context, span_len):
    row_count = queries.shape[0]
    head_count = queries.shape[1]
    head_size = queries.shape[2]
    key_count = keys_all.shape[0]
    block_rows = math.gcd(row_count, 256)
    scale = 1.0 / math.sqrt(head_size)

    def kernel(context_ref, query_ref, key_ref, value_ref, out_ref):
        scores = (
            lax.dot_general(
                query_ref[...],
                key_ref[...],
                (((1,), (1,)), ((), ())),
                preferred_element_type=jnp.float32,
            )
            * scale
        )
        key_pos = lax.broadcasted_iota(jnp.int32, scores.shape, 1)
        query_pos = pl.program_id(1) * block_rows + lax.broadcasted_iota(
            jnp.int32, scores.shape, 0
        )
        cached = key_pos < span_len
        allowed = (cached & (key_pos < context_ref[0])) | (
            jnp.logical_not(cached) & (key_pos - span_len <= query_pos)
        )
        scores = jnp.where(allowed, scores, -1e30)
        largest = jnp.max(scores, axis=-1, keepdims=True)
        weights = jnp.where(allowed, jnp.exp(scores - largest), 0.0)
        probs = (weights / jnp.sum(weights, axis=-1, keepdims=True)).astype(jnp.bfloat16)
        out_ref[...] = jnp.dot(probs, value_ref[...], preferred_element_type=jnp.float32).astype(
            jnp.bfloat16
        )

    width = head_count * head_size
    result = pl.pallas_call(
        kernel,
        out_shape=jax.ShapeDtypeStruct((row_count, width), jnp.bfloat16),
        grid_spec=pltpu.PrefetchScalarGridSpec(
            num_scalar_prefetch=1,
            grid=(head_count, row_count // block_rows),
            in_specs=[
                pl.BlockSpec((block_rows, head_size), lambda h, i, c: (i, h)),
                pl.BlockSpec((key_count, head_size), lambda h, i, c: (0, h)),
                pl.BlockSpec((key_count, head_size), lambda h, i, c: (0, h)),
            ],
            out_specs=pl.BlockSpec((block_rows, head_size), lambda h, i, c: (i, h)),
        ),
    )(
        jnp.reshape(context, (1,)).astype(jnp.int32),
        queries.reshape(row_count, width),
        keys_all.reshape(key_count, width),
        values_all.reshape(key_count, width),
    )
    return result


def per_device(
    hidden_in,
    context_len,
    page_table,
    paged_cache,
    attn_gain,
    proj_weight,
    proj_bias,
    out_weight,
    mlp_gain,
    expert_ids,
    route_weight,
    w_experts_in,
    w_experts_out,
    w_shared_in,
    w_shared_out,
    shared_gate,
):
    tok_rows = hidden_in.shape[0]
    width = hidden_in.shape[1]
    head_lanes = lax.axis_size(HEAD)
    device_count = lax.axis_size("tok") * head_lanes
    expert_count = device_count // 2
    top_count = expert_ids.shape[1]
    capacity = 2 * max(1, tok_rows * top_count * 5 // (8 * expert_count))
    gathered = lax.all_gather(hidden_in, HEAD, axis=0, tiled=True)
    stretch_rows = gathered.shape[0]
    heads_here = proj_weight.shape[2] // HD
    normed = rms_scale(gathered, attn_gain)
    projected = (
        jnp.einsum("td,cdf->ctf", normed, proj_weight, preferred_element_type=jnp.float32)
        + proj_bias.astype(jnp.float32)[:, None, :]
    )
    context = context_len[0]
    positions = context + jnp.arange(stretch_rows, dtype=jnp.int32)
    queries = rotate(projected[0].reshape(stretch_rows, heads_here, HD), positions).astype(
        jnp.bfloat16
    )
    new_keys = rotate(projected[1].reshape(stretch_rows, heads_here, HD), positions).astype(
        jnp.bfloat16
    )
    new_values = projected[2].reshape(stretch_rows, heads_here, HD).astype(jnp.bfloat16)
    ordered = jnp.take(paged_cache, page_table[0], axis=1)
    span_len = ordered.shape[1] * ordered.shape[2]
    ordered = ordered.reshape(2, span_len, heads_here, HD)
    keys_all = jnp.concatenate([ordered[0], new_keys], axis=0)
    values_all = jnp.concatenate([ordered[1], new_values], axis=0)
    heads_out = attend(queries, keys_all, values_all, context, span_len).reshape(
        stretch_rows, heads_here * HD
    )
    attn_own = lax.psum_scatter(
        jnp.dot(heads_out, out_weight, preferred_element_type=jnp.float32).astype(jnp.bfloat16),
        HEAD,
        scatter_dimension=0,
        tiled=True,
    ).astype(jnp.float32)
    resid = (hidden_in.astype(jnp.float32) + attn_own).astype(jnp.bfloat16)
    mixed = rms_scale(resid, mlp_gain)
    inner = jnp.einsum(
        "td,dcf->tcf",
        lax.all_gather(mixed, HEAD, axis=0, tiled=True),
        w_shared_in,
        preferred_element_type=jnp.float32,
    )
    activated = (jax.nn.silu(inner[:, 0]) * inner[:, 1]).astype(jnp.bfloat16)
    shared_part = jnp.dot(activated, w_shared_out, preferred_element_type=jnp.float32)
    shared_own = lax.psum_scatter(
        shared_part.astype(jnp.bfloat16), HEAD, scatter_dimension=0, tiled=True
    ).astype(jnp.float32)
    gate = jax.nn.sigmoid(jnp.dot(mixed, shared_gate, preferred_element_type=jnp.float32))
    flat_ids = expert_ids.reshape(-1)
    one_hot = (flat_ids[:, None] == jnp.arange(expert_count, dtype=jnp.int32)[None, :]).astype(
        jnp.int32
    )
    earlier = jnp.cumsum(one_hot, axis=0) - one_hot
    slot_pos = jnp.sum(earlier * one_hot, axis=1)
    slot_index = flat_ids * capacity + slot_pos
    slot_table = slot_index.reshape(tok_rows, top_count)
    dispatch_matrix = jnp.sum(
        (
            jnp.arange(expert_count * capacity, dtype=jnp.int32)[:, None, None] == slot_table[None]
        ).astype(jnp.int32),
        axis=2,
    ).astype(jnp.bfloat16)
    buffer = jnp.dot(dispatch_matrix, mixed, preferred_element_type=jnp.float32).astype(
        jnp.bfloat16
    )
    pair = [(0, 1), (1, 0)]
    arrived = lax.all_to_all(buffer, ("tok", "x"), 0, 0, tiled=True)
    sibling = lax.ppermute(arrived, "core", pair)

    def half_expert(rows):
        inner = jnp.dot(rows, w_experts_in[0], preferred_element_type=jnp.float32)
        middle = inner.shape[1] // 2
        activated = (jax.nn.silu(inner[:, :middle]) * inner[:, middle:]).astype(jnp.bfloat16)
        return jnp.dot(activated, w_experts_out[0], preferred_element_type=jnp.float32).astype(
            jnp.bfloat16
        )

    part_own = half_expert(arrived)
    part_back = lax.ppermute(half_expert(sibling), "core", pair)
    merged_own = (part_own.astype(jnp.float32) + part_back.astype(jnp.float32)).astype(
        jnp.bfloat16
    )
    merged = lax.all_to_all(merged_own, ("tok", "x"), 0, 0, tiled=True)
    combine = jnp.sum(
        jnp.where(
            jnp.arange(expert_count * capacity, dtype=jnp.int32)[None, None, :]
            == slot_table[:, :, None],
            route_weight[:, :, None],
            0.0,
        ),
        axis=1,
    )
    routed = jnp.dot(
        combine,
        merged.astype(jnp.float32),
        precision=lax.Precision.HIGHEST,
        preferred_element_type=jnp.float32,
    )
    return (resid.astype(jnp.float32) + gate[:, None] * shared_own + routed).astype(jnp.bfloat16)


def solution(mesh):
    split = Mesh(
        mesh.devices.reshape(mesh.shape["tok"], mesh.shape["head"] // 2, 2), ("tok", "x", "core")
    )
    in_specs = (
        P(ROWS, None),
        P("tok"),
        P("tok", None),
        P(None, "tok", None, HEAD),
        P(),
        P(None, None, HEAD),
        P(None, HEAD),
        P(HEAD, None),
        P(),
        P(ROWS, None),
        P(ROWS, None),
        P(ROWS, None, None),
        P(ROWS, None, None),
        P(None, None, HEAD),
        P(HEAD, None),
        P(),
    )
    out_specs = P(ROWS, None)
    return jax.shard_map(
        per_device, mesh=split, in_specs=in_specs, out_specs=out_specs, check_vma=False
    )
```

profile of v0, /device:TPU:1, one launch (start us, length us, event | category | flops | bytes accessed | tf_op | source)
XLA Modules:
  0.0 326.6 jit_solution(15679627499058347059)
XLA Ops:
  10.2 3.6 %gather_fusion = bf16[16,2,128,256]{3,2,1,0:T(8,128)(2,1)} fusion(bf16[2,16,128,256]{3,2,1,0:T(8,128)(2,1)} %param.19, s32[1024]{0:T(1024)S(1)} %pad_clamp_fusion), kind=kCustom, calls=%fused_computation | custom fusion | bytes 4194368 | tf_op jit(solution)/shard_map/jit(_take)/gather | solution.py:133
  14.0 2.9 fusion.42
  17.2 1.5 fusion.53
  18.7 26.0 %all-gather.3.cloned.1.call-done = bf16[1024,2048]{1,0:T(8,128)(2,1)} async-done(((bf16[128,2048]{1,0:T(8,128)(2,1)}), bf16[1024,2048]{1,0:T(8,128)(2,1)}) %all-gather.3.cloned.1.call-update) | async-done | bytes 4194320 | tf_op jit(solution)/shard_map/all_gather | solution.py:116
  44.7 3.2 fusion
  48.1 3.5 %add_bitcast_fusion = f32[3,1024,256]{2,1,0:T(8,128)S(1)} fusion(bf16[3,2048,256]{2,1,0:T(8,128)(2,1)S(1)} %copy-done, bf16[1024,2048]{1,0:T(8,128)(2,1)S(1)} %copy-done.7, f32[2048]{0:T(1024)S(1)} %convert_element_type.107, f32[1024]{0:T(1024)S(1)} %add_rsqrt_fusion, f32[3,256]{1,0:T(4,128)S(1)} %convert_element_type.109), kind=kOutput, calls=%fused_computation.22 | convolution fusion | flops 3230400512 | bytes 10501120 | tf_op jit(solution)/shard_map/td,cdf->ctf/dot_general | solution.py:121
  54.5 2.3 slice_negate_fusion
  56.8 2.3 maximum_multiply_fusion.1
  59.6 1.2 fusion.34
  60.8 1.3 pad_maximum_fusion.key_ref
  62.7 1.2 pad_maximum_fusion.1.value_ref
  64.0 17.6 %shard_map.154 = bf16[1024,256]{1,0:T(8,128)(2,1)} custom-call(s32[1]{0:T(128)} %copy.56.context_ref, bf16[1024,256]{1,0:T(8,128)(2,1)} %get-tuple-element.6.query_ref, bf16[3072,256]{1,0:T(8,128)(2,1)} %pad_maximum_fusion.key_ref, bf16[3072,256]{1,0:T(8,128)(2,1)} %pad_maximum_fusion.1.value_ref), custom_call_target="tpu_custom_call" | custom-call | tf_op jit(solution)/shard_map/pallas_call | solution.py:69
  81.6 4.2 %convolution_convert_fusion.1 = bf16[1024,2048]{1,0:T(8,128)(2,1)} fusion(bf16[1024,256]{1,0:T(8,128)(2,1)} %shard_map.154, bf16[256,2048]{1,0:T(8,128)(2,1)S(1)} %copy-done.13), kind=kOutput, calls=%fused_computation.18 | convolution fusion | flops 1075838976 | bytes 5767168 | tf_op jit(solution)/shard_map/dot_general | solution.py:142
  86.5 34.1 %reduce-scatter.3.cloned.1.call-done = bf16[128,2048]{1,0:T(8,128)(2,1)} async-done(((bf16[1024,2048]{1,0:T(8,128)(2,1)}), bf16[128,2048]{1,0:T(8,128)(2,1)}) %reduce-scatter.3.cloned.1.call-update) | async-done | bytes 524304 | tf_op jit(solution)/shard_map/reduce_scatter | solution.py:141
  120.6 1.3 fusion.31
  121.9 2.0 fusion.33
  124.4 1.2 reduce-window.6
  126.4 1.9 convolution_convert_fusion.4
  128.2 2.8 all_to_all.16
  131.0 75.4 %all_to_all.24 = bf16[64,10,2048]{2,1,0:T(8,128)(2,1)} all-to-all(bf16[64,10,2048]{2,1,0:T(8,128)(2,1)} %all_to_all.16), channel_id=1, replica_groups=mesh['tok'=16,'x'=4,'core'=2] {'tok','x'}, dimensions={0} | all-to-all | bytes 5242880 | tf_op jit(solution)/shard_map/all_to_all | solution.py:179
  206.4 4.1 %all_to_all.18 = bf16[640,2048]{1,0:T(8,128)(2,1)S(1)} reshape(bf16[64,10,2048]{2,1,0:T(8,128)(2,1)} %all_to_all.24) | data formatting | bytes 5242880 | tf_op jit(solution)/shard_map/all_to_all | solution.py:179
  211.6 9.6 %fusion.10 = f32[1024,2,704]{0,2,1:T(8,128)S(1)} fusion(bf16[2048,2,704]{0,2,1:T(8,128)(2,1)} %param.29, bf16[1024,2048]{1,0:T(8,128)(2,1)} %all-gather.5.cloned.1.call-done), kind=kOutput, calls=%fused_computation.13 | convolution fusion | flops 5905580032 | bytes 15728640 | tf_op jit(solution)/shard_map/td,dcf->tcf/dot_general | solution.py:149
  221.2 5.3 %convolution_convert_fusion = bf16[1024,2048]{1,0:T(8,128)(2,1)} fusion(bf16[704,2048]{1,0:T(8,128)(2,1)S(1)} %copy-done.18, f32[1024,2,704]{0,2,1:T(8,128)S(1)} %fusion.10), kind=kOutput, calls=%fused_computation.17 | convolution fusion | flops 2959212544 | bytes 12845056 | tf_op jit(solution)/shard_map/dot_general | solution.py:156
  226.5 7.5 %fusion.3 = f32[640,1408]{1,0:T(8,128)S(1)} fusion(bf16[640,2048]{1,0:T(8,128)(2,1)} %collective-permute-done, bf16[1,2048,1408]{2,1,0:T(8,128)(2,1)} %param.27), kind=kOutput, calls=%fused_computation.6 | convolution fusion | flops 3690987520 | bytes 11993088 | tf_op jit(solution)/shard_map/dot_general | solution.py:183
  234.1 2.3 convolution_convert_fusion.2
  236.7 6.7 %fusion.5 = f32[640,1408]{1,0:T(8,128)S(1)} fusion(bf16[640,2048]{1,0:T(8,128)(2,1)S(1)} %all_to_all.18, bf16[1,2048,1408]{2,1,0:T(8,128)(2,1)} %param.27), kind=kOutput, calls=%fused_computation.8 | convolution fusion | flops 3690987520 | bytes 11993088 | tf_op jit(solution)/shard_map/dot_general | solution.py:183
  243.4 2.3 add_convert_fusion
  245.8 2.9 all_to_all.19
  248.6 5.8 %all-to-all-start.1 = ((bf16[64,10,2048]{2,1,0:T(8,128)(2,1)}), bf16[64,10,2048]{2,1,0:T(8,128)(2,1)}, u32[]{:S(2)}, u32[]{:S(2)}) async-start(bf16[64,10,2048]{2,1,0:T(8,128)(2,1)} %all_to_all.19), calls=%async_computation.3 | async-start | bytes 8388608 | tf_op jit(solution)/shard_map/all_to_all | solution.py:195
  254.9 55.1 %all-to-all-done.1 = bf16[64,10,2048]{2,1,0:T(8,128)(2,1)} async-done(((bf16[64,10,2048]{2,1,0:T(8,128)(2,1)}), bf16[64,10,2048]{2,1,0:T(8,128)(2,1)}, u32[]{:S(2)}, u32[]{:S(2)}) %all-to-all-start.1) | async-done | bytes 2621472 | tf_op jit(solution)/shard_map/all_to_all | solution.py:195
  310.1 5.7 %all_to_all.21 = bf16[640,2048]{1,0:T(8,128)(2,1)} reshape(bf16[64,10,2048]{2,1,0:T(8,128)(2,1)} %all-to-all-done.1) | data formatting | bytes 5242880 | tf_op jit(solution)/shard_map/all_to_all | solution.py:195
  315.7 4.4 %fusion.20 = bf16[128,2048]{1,0:T(8,128)(2,1)} fusion(f32[128,640]{1,0:T(8,128)S(1)} %select_reduce_fusion, bf16[640,2048]{1,0:T(8,128)(2,1)} %all_to_all.21, bf16[128,2048]{1,0:T(8,128)(2,1)} %reduce-scatter.5.cloned.1.call-done, f32[128]{0:T(128)S(1)} %fusion.30, bf16[128,2048]{1,0:T(8,128)(2,1)} %reduce-scatter.3.cloned.1.call-done, ...), kind=kOutput, calls=%fused_computation.30 | convolution fusion | flops 2015887360 | bytes 5046784 | tf_op jit(solution)/shard_map/dot_general | solution.py:205
  (88 shorter events, 11.3 us)
Async XLA Ops:
  6.5 41.4 %copy-start = (bf16[3,2048,256]{2,1,0:T(8,128)(2,1)S(1)}, bf16[3,2048,256]{2,1,0:T(8,128)(2,1)}, u32[]{:S(2)}) copy-start(bf16[3,2048,256]{2,1,0:T(8,128)(2,1)} %param.21) | copy-start | bytes 9437188
  6.5 38.2 %all-gather.3.cloned.1.call-start = ((), (), s32[]{:S(2)}) async-start(), calls=%async_computation.4 | async-start | bytes 4718592 | tf_op jit(solution)/shard_map/all_gather | solution.py:116
  7.3 113.4 %reduce-scatter.3.cloned.1.call-start = ((), (), s32[]{:S(2)}) async-start(), calls=%async_computation.5 | async-start | bytes 4718592 | tf_op jit(solution)/shard_map/reduce_scatter | solution.py:141
  10.2 6.7 %copy-start.20 = (s32[1,16]{1,0:T(1,128)S(1)}, s32[1,16]{1,0:T(1,128)}, u32[]{:S(2)}) copy-start(s32[1,16]{1,0:T(1,128)} %param.18) | copy-start | bytes 196
  13.8 3.1 copy-start.2
  44.7 3.4 %copy-start.7 = (bf16[1024,2048]{1,0:T(8,128)(2,1)S(1)}, bf16[1024,2048]{1,0:T(8,128)(2,1)}, u32[]{:S(2)}) copy-start(bf16[1024,2048]{1,0:T(8,128)(2,1)} %all-gather.3.cloned.1.call-done) | copy-start | bytes 12582916
  51.6 1.8 copy-start.5
  54.5 2.3 copy-start.12
  56.8 2.4 copy-start.10
  56.8 2.7 copy-start.6
  59.6 1.2 copy-start.9
  60.8 1.7 copy-start.8
  60.8 1.9 copy-start.11
  64.0 17.6 %copy-start.13 = (bf16[256,2048]{1,0:T(8,128)(2,1)S(1)}, bf16[256,2048]{1,0:T(8,128)(2,1)}, u32[]{:S(2)}) copy-start(bf16[256,2048]{1,0:T(8,128)(2,1)} %param.23) | copy-start | bytes 3145732
  85.8 0.7 copy-start.15
  85.8 34.8 %copy-start.4 = (bf16[128,2048]{1,0:T(8,128)(2,1)S(1)}, bf16[128,2048]{1,0:T(8,128)(2,1)}, u32[]{:S(2)}) copy-start(bf16[128,2048]{1,0:T(8,128)(2,1)} %param.16) | copy-start | bytes 1572868
  85.8 38.2 %copy-start.14 = (s32[128,4]{0,1:T(4,128)S(1)}, s32[128,4]{0,1:T(4,128)}, u32[]{:S(2)}) copy-start(s32[128,4]{0,1:T(4,128)} %param.25) | copy-start | bytes 6148
  85.8 125.8 %all-gather.5.cloned.1.call-start = ((), (), s32[]{:S(2)}) async-start(), calls=%async_computation.6 | async-start | bytes 4718592 | tf_op jit(solution)/shard_map/all_gather | solution.py:151
  124.0 191.7 %reduce-scatter.5.cloned.1.call-start = ((), (), s32[]{:S(2)}) async-start(), calls=%async_computation.7 | async-start | bytes 4718592 | tf_op jit(solution)/shard_map/reduce_scatter | solution.py:157
  210.5 16.0 %collective-permute-start = (bf16[640,2048]{1,0:T(8,128)(2,1)S(1)}, bf16[640,2048]{1,0:T(8,128)(2,1)}, u32[]{:S(2)}, u32[]{:S(2)}) collective-permute-start(bf16[640,2048]{1,0:T(8,128)(2,1)S(1)} %all_to_all.18), channel_id=1, source_target_pairs={{0,1},{1,0},{2,3},{3,2},{4,5},{5,4},{6,7},{7,6},{8,9},{9,8},{10,11... | collective-permute-start | bytes 7864328 | tf_op jit(solution)/shard_map/ppermute | solution.py:180
  211.6 9.6 %copy-start.18 = (bf16[704,2048]{1,0:T(8,128)(2,1)S(1)}, bf16[704,2048]{1,0:T(8,128)(2,1)}, u32[]{:S(2)}) copy-start(bf16[704,2048]{1,0:T(8,128)(2,1)} %param.30) | copy-start | bytes 8650756
  226.5 7.6 %copy-start.19 = (bf16[1,704,2048]{2,1,0:T(8,128)(2,1)S(1)}, bf16[1,704,2048]{2,1,0:T(8,128)(2,1)}, u32[]{:S(2)}) copy-start(bf16[1,704,2048]{2,1,0:T(8,128)(2,1)} %param.28) | copy-start | bytes 8650756
  236.4 7.0 %collective-permute-start.1 = (bf16[640,2048]{1,0:T(8,128)(2,1)S(1)}, bf16[640,2048]{1,0:T(8,128)(2,1)S(1)}, u32[]{:S(2)}, u32[]{:S(2)}) collective-permute-start(bf16[640,2048]{1,0:T(8,128)(2,1)S(1)} %convolution_convert_fusion.2), channel_id=1, source_target_pairs={{0,1},{1,0},{2,3},{3,2},{4,5},{5,4},{6,7},{7,6},{8,9},{9,8},{10,11... | collective-permute-start | bytes 7864328 | tf_op jit(solution)/shard_map/ppermute | solution.py:191
  248.6 5.8 %copy-start.16 = (bf16[2048]{0:T(1024)(128)(2,1)S(1)}, bf16[2048]{0:T(1024)(128)(2,1)}, u32[]{:S(2)}) copy-start(bf16[2048]{0:T(1024)(128)(2,1)} %param.31) | copy-start | bytes 12292
  248.6 5.8 %copy-start.17 = (f32[128,4]{0,1:T(4,128)S(1)}, f32[128,4]{0,1:T(4,128)}, u32[]{:S(2)}) copy-start(f32[128,4]{0,1:T(4,128)} %param.26) | copy-start | bytes 6148
  248.6 6.0 %copy-start.3 = (bf16[128,2048]{1,0:T(8,128)(2,1)S(1)}, bf16[128,2048]{1,0:T(8,128)(2,1)}, u32[]{:S(2)}) copy-start(bf16[128,2048]{1,0:T(8,128)(2,1)} %fusion.33) | copy-start | bytes 1572868
  248.6 61.4 %all-to-all-start.1 = ((bf16[64,10,2048]{2,1,0:T(8,128)(2,1)}), bf16[64,10,2048]{2,1,0:T(8,128)(2,1)}, u32[]{:S(2)}, u32[]{:S(2)}) async-start(bf16[64,10,2048]{2,1,0:T(8,128)(2,1)} %all_to_all.19), calls=%async_computation.3 | async-start | bytes 8388608 | tf_op jit(solution)/shard_map/all_to_all | solution.py:195
  310.1 10.0 %copy-start.1 = (bf16[3,2048,256]{2,1,0:T(8,128)(2,1)S(1)}, bf16[3,2048,256]{2,1,0:T(8,128)(2,1)}, u32[]{:S(2)}) copy-start(bf16[3,2048,256]{2,1,0:T(8,128)(2,1)} %param.21) | copy-start | bytes 9437188
Sparse Core Ops, SparseCore 0:
  9.0 35.6 all-gather.2
  86.0 34.6 reduce-scatter.2
  124.1 56.5 all-gather.4
  226.6 29.5 reduce-scatter.4
where the time goes:
time: 328 us; the launch traced here: 327 us
  waiting for transfers between devices  116 us (35%)
  blocking collectives  75.4 us (23%)
  matrix products  47.9 us (15%)
  local copies, waits for them, and re-layouts  26 us (8%)
  other arithmetic  22.3 us (7%)
  Pallas kernels  17.6 us (5%)
  between operations  14.1 us (4%)
  starting transfers between devices  7.34 us (2%)
    all_to_all x1, blocking collectives, per_device(): arrived = lax.all_to_all(buffer, ('tok', 'x'), 0, 0, tiled=True)  75.4 us
    all_to_all x1, waiting for transfers between devices, per_device(): merged = lax.all_to_all(merged_own, ('tok', 'x'), 0, 0, tiled=True)  55.1 us
    reduce_scatter x1, waiting for transfers between devices, per_device(): lax.psum_scatter(jnp.dot(heads_out, out_weight, preferred_element_type=jn...  34.1 us
    all_gather x1, waiting for transfers between devices, per_device(): gathered = lax.all_gather(hidden_in, HEAD, axis=0, tiled=True)  26 us
    pallas_call x1, Pallas kernels, attend(): pl.pallas_call(kernel, out_shape=jax.ShapeDtypeStruct((row_count, width),...  17.6 us
    dot_general x2, matrix products, half_expert(): inner = jnp.dot(rows, w_experts_in[0], preferred_element_type=jnp.float32)  14.2 us
    dot_general x1, matrix products, per_device(): jnp.einsum('td,dcf->tcf', lax.all_gather(mixed, HEAD, axis=0, tiled=True)...  9.59 us
    all_to_all x2, local copies, waits for them, and re-layouts, per_device(): merged = lax.all_to_all(merged_own, ('tok', 'x'), 0, 0, tiled=True)  8.54 us
  transfers between devices with their start and end apart: 7, of which 3 were waited for; matrix products, arithmetic and copies ran while one was open for 15% of the time, Pallas kernels for 0%

commit v1 on v0

--- a/solution.py
+++ b/solution.py
@@ -176,7 +176,10 @@
         jnp.bfloat16
     )
     pair = [(0, 1), (1, 0)]
-    arrived = lax.all_to_all(buffer, ("tok", "x"), 0, 0, tiled=True)
+    tiles = (expert_count, capacity, width // 128, 128)
+    arrived = lax.all_to_all(buffer.reshape(tiles), ("tok", "x"), 0, 0, tiled=True).reshape(
+        expert_count * capacity, width
+    )
     sibling = lax.ppermute(arrived, "core", pair)
 
     def half_expert(rows):
@@ -192,7 +195,9 @@
     merged_own = (part_own.astype(jnp.float32) + part_back.astype(jnp.float32)).astype(
         jnp.bfloat16
     )
-    merged = lax.all_to_all(merged_own, ("tok", "x"), 0, 0, tiled=True)
+    merged = lax.all_to_all(merged_own.reshape(tiles), ("tok", "x"), 0, 0, tiled=True).reshape(
+        expert_count * capacity, width
+    )
     combine = jnp.sum(
         jnp.where(
             jnp.arange(expert_count * capacity, dtype=jnp.int32)[None, None, :]

time: 328 us -> 284 us (0.87)
  waiting for transfers between devices: 116 us -> 97.4 us
  blocking collectives: 75.4 us -> 60 us
  local copies, waits for them, and re-layouts: 26 us -> 15.9 us
    all_to_all x1, waiting for transfers between devices: 55.1 us -> 36.5 us  [per_device(): lax.all_to_all(merged_own.reshape(tiles), ('tok', 'x'), 0, 0, tiled=True)]
    all_to_all x4 -> x0, local copies, waits for them, and re-layouts: 15.4 us -> none  [the longest x2 8.54 us: per_device(): merged = lax.all_to_all(merged_own, ('tok', 'x'), 0, 0, tiled=True)]
    all_to_all x1, blocking collectives: 75.4 us -> 60 us  [per_device(): lax.all_to_all(buffer.reshape(tiles), ('tok', 'x'), 0, 0, tiled=True)]
    unnamed x44 -> x45, local copies, waits for them, and re-layouts: 2.24 us -> 7.65 us
  transfers between devices with their start and end apart: 7 -> 7, of which waited for: 3 -> 3; matrix products, arithmetic and copies ran while one was open for 15% -> 20% of each run, Pallas kernels for 0% -> 0%
where the time goes in v1:
time: 284 us
  waiting for transfers between devices  97.4 us (34%)
  blocking collectives  60 us (21%)
  matrix products  49.3 us (17%)
  other arithmetic  22.3 us (8%)
  Pallas kernels  17.6 us (6%)
  local copies, waits for them, and re-layouts  15.9 us (6%)
  between operations  14.1 us (5%)
  starting transfers between devices  7.13 us (3%)
    all_to_all x1, blocking collectives, per_device(): lax.all_to_all(buffer.reshape(tiles), ('tok', 'x'), 0, 0, tiled=True)  60 us
    all_to_all x1, waiting for transfers between devices, per_device(): lax.all_to_all(merged_own.reshape(tiles), ('tok', 'x'), 0, 0, tiled=True)  36.5 us
    reduce_scatter x1, waiting for transfers between devices, per_device(): lax.psum_scatter(jnp.dot(heads_out, out_weight, preferred_element_type=jn...  34.1 us
    all_gather x1, waiting for transfers between devices, per_device(): gathered = lax.all_gather(hidden_in, HEAD, axis=0, tiled=True)  26.1 us
    pallas_call x1, Pallas kernels, attend(): pl.pallas_call(kernel, out_shape=jax.ShapeDtypeStruct((row_count, width),...  17.6 us
    dot_general x2, matrix products, half_expert(): inner = jnp.dot(rows, w_experts_in[0], preferred_element_type=jnp.float32)  14.3 us
    dot_general x1, matrix products, per_device(): jnp.einsum('td,dcf->tcf', lax.all_gather(mixed, HEAD, axis=0, tiled=True)...  9.59 us
    unnamed x45, local copies, waits for them, and re-layouts  7.65 us
  transfers between devices with their start and end apart: 7, of which 3 were waited for; matrix products, arithmetic and copies ran while one was open for 20% of the time, Pallas kernels for 0%

profile of v1, /device:TPU:1, one launch (start us, length us, event | category | flops | bytes accessed | tf_op | source)
XLA Modules:
  0.0 283.8 jit_solution(570639148265853368)
XLA Ops:
  10.2 3.6 %gather_fusion = bf16[16,2,128,256]{3,2,1,0:T(8,128)(2,1)} fusion(bf16[2,16,128,256]{3,2,1,0:T(8,128)(2,1)} %param.19, s32[1024]{0:T(1024)S(1)} %pad_clamp_fusion), kind=kCustom, calls=%fused_computation | custom fusion | bytes 4194368 | tf_op jit(solution)/shard_map/jit(_take)/gather | solution.py:133
  14.0 2.9 %fusion.52 = (f32[1024,128]{1,0:T(8,128)}, f32[1024,128]{1,0:T(8,128)}) fusion(f32[1024,64]{1,0:T(8,128)S(1)} %broadcast_multiply_fusion), kind=kLoop, calls=%fused_computation.77 | loop fusion | flops 131072 | bytes 1310720 | tf_op jit(solution)/shard_map/cos | solution.py:31
  17.2 1.5 fusion.63
  18.6 26.1 %all-gather.3.cloned.1.call-done = bf16[1024,2048]{1,0:T(8,128)(2,1)} async-done(((bf16[128,2048]{1,0:T(8,128)(2,1)}), bf16[1024,2048]{1,0:T(8,128)(2,1)}) %all-gather.3.cloned.1.call-update) | async-done | bytes 4194320 | tf_op jit(solution)/shard_map/all_gather | solution.py:116
  44.7 3.2 %fusion = f32[1024]{0:T(1024)S(1)} fusion(bf16[1024,2048]{1,0:T(8,128)(2,1)} %all-gather.3.cloned.1.call-done), kind=kLoop, calls=%fused_computation.3 | loop fusion | flops 6290432 | bytes 4198400 | tf_op jit(solution)/shard_map/reduce_sum | solution.py:21
  48.1 3.5 %add_bitcast_fusion = f32[3,1024,256]{2,1,0:T(8,128)S(1)} fusion(bf16[3,2048,256]{2,1,0:T(8,128)(2,1)S(1)} %copy-done, bf16[1024,2048]{1,0:T(8,128)(2,1)S(1)} %copy-done.6, f32[2048]{0:T(1024)S(1)} %convert_element_type.107, f32[1024]{0:T(1024)S(1)} %add_rsqrt_fusion, f32[3,256]{1,0:T(4,128)S(1)} %convert_element_type.109), kind=kOutput, calls=%fused_computation.22 | convolution fusion | flops 3230400512 | bytes 10501120 | tf_op jit(solution)/shard_map/td,cdf->ctf/dot_general | solution.py:121
  51.8 1.0 fusion.50
  54.5 2.3 slice_negate_fusion
  56.8 2.3 maximum_multiply_fusion.1
  59.6 1.2 fusion.44
  60.8 1.3 pad_maximum_fusion.key_ref
  62.7 1.3 pad_maximum_fusion.1.value_ref
  64.0 17.6 %shard_map.154 = bf16[1024,256]{1,0:T(8,128)(2,1)} custom-call(s32[1]{0:T(128)} %copy.71.context_ref, bf16[1024,256]{1,0:T(8,128)(2,1)} %get-tuple-element.6.query_ref, bf16[3072,256]{1,0:T(8,128)(2,1)} %pad_maximum_fusion.key_ref, bf16[3072,256]{1,0:T(8,128)(2,1)} %pad_maximum_fusion.1.value_ref), custom_call_target="tpu_custom_call" | custom-call | tf_op jit(solution)/shard_map/pallas_call | solution.py:69
  81.6 4.3 %convolution_convert_fusion.1 = bf16[1024,2048]{1,0:T(8,128)(2,1)} fusion(bf16[1024,256]{1,0:T(8,128)(2,1)} %shard_map.154, bf16[256,2048]{1,0:T(8,128)(2,1)S(1)} %copy-done.12), kind=kOutput, calls=%fused_computation.18 | convolution fusion | flops 1075838976 | bytes 5767168 | tf_op jit(solution)/shard_map/dot_general | solution.py:142
  86.5 34.1 %reduce-scatter.3.cloned.1.call-done = bf16[128,2048]{1,0:T(8,128)(2,1)} async-done(((bf16[1024,2048]{1,0:T(8,128)(2,1)}), bf16[128,2048]{1,0:T(8,128)(2,1)}) %reduce-scatter.3.cloned.1.call-update) | async-done | bytes 524304 | tf_op jit(solution)/shard_map/reduce_scatter | solution.py:141
  120.6 1.3 fusion.41
  121.9 2.0 fusion.43
  124.4 1.2 reduce-window.6
  126.4 1.9 fusion.32
  129.1 60.0 %all_to_all.10 = bf16[64,10,16,128]{3,2,1,0:T(8,128)(2,1)S(1)} all-to-all(bf16[64,10,16,128]{3,2,1,0:T(8,128)(2,1)S(1)} %bitcast.134), channel_id=1, replica_groups=mesh['tok'=16,'x'=4,'core'=2] {'tok','x'}, dimensions={0} | all-to-all | bytes 5242880 | tf_op jit(solution)/shard_map/all_to_all | solution.py:180
  189.1 2.2 copy.70
  192.3 9.6 %fusion.10 = f32[1024,2,704]{0,2,1:T(8,128)S(1)} fusion(bf16[2048,2,704]{0,2,1:T(8,128)(2,1)} %param.29, bf16[1024,2048]{1,0:T(8,128)(2,1)} %all-gather.5.cloned.1.call-done), kind=kOutput, calls=%fused_computation.13 | convolution fusion | flops 5905580032 | bytes 15728640 | tf_op jit(solution)/shard_map/td,dcf->tcf/dot_general | solution.py:149
  201.9 5.3 %convolution_convert_fusion = bf16[1024,2048]{1,0:T(8,128)(2,1)} fusion(bf16[704,2048]{1,0:T(8,128)(2,1)S(1)} %copy-done.17, f32[1024,2,704]{0,2,1:T(8,128)S(1)} %fusion.10), kind=kOutput, calls=%fused_computation.17 | convolution fusion | flops 2959212544 | bytes 12845056 | tf_op jit(solution)/shard_map/dot_general | solution.py:156
  207.3 7.5 %fusion.3 = f32[640,1408]{1,0:T(8,128)S(1)} fusion(bf16[640,2048]{1,0:T(8,128)(2,1)} %collective-permute-done, bf16[1,2048,1408]{2,1,0:T(8,128)(2,1)} %param.27), kind=kOutput, calls=%fused_computation.6 | convolution fusion | flops 3690987520 | bytes 11993088 | tf_op jit(solution)/shard_map/dot_general | solution.py:186
  214.8 2.3 convolution_convert_fusion.2
  217.4 6.7 %fusion.5 = f32[640,1408]{1,0:T(8,128)S(1)} fusion(bf16[1,2048,1408]{2,1,0:T(8,128)(2,1)} %param.27, bf16[80,8,16,128]{3,2,1,0:T(8,128)(2,1)S(1)} %bitcast.133), kind=kOutput, calls=%fused_computation.8 | convolution fusion | flops 3690987520 | bytes 11993088 | tf_op jit(solution)/shard_map/dot_general | solution.py:186
  224.2 2.4 fusion.18
  226.6 2.4 copy.53
  229.0 5.7 %all-to-all-start.1 = ((bf16[64,10,16,128]{3,2,1,0:T(8,128)(2,1)}), bf16[64,10,16,128]{3,2,1,0:T(8,128)(2,1)}, u32[]{:S(2)}, u32[]{:S(2)}) async-start(bf16[64,10,16,128]{3,2,1,0:T(8,128)(2,1)} %bitcast.35), calls=%async_computation.3 | async-start | bytes 5242880 | tf_op jit(solution)/shard_map/all_to_all | solution.py:198
  234.9 1.4 fusion.40
  236.4 36.5 %all-to-all-done.1 = bf16[64,10,16,128]{3,2,1,0:T(8,128)(2,1)} async-done(((bf16[64,10,16,128]{3,2,1,0:T(8,128)(2,1)}), bf16[64,10,16,128]{3,2,1,0:T(8,128)(2,1)}, u32[]{:S(2)}, u32[]{:S(2)}) %all-to-all-start.1) | async-done | bytes 2621472 | tf_op jit(solution)/shard_map/all_to_all | solution.py:198
  272.8 4.5 %fusion.27 = bf16[128,2048]{1,0:T(8,128)(2,1)} fusion(f32[128,640]{1,0:T(8,128)S(1)} %select_reduce_fusion, bf16[80,8,16,128]{3,2,1,0:T(8,128)(2,1)} %bitcast.37, bf16[128,2048]{1,0:T(8,128)(2,1)} %reduce-scatter.5.cloned.1.call-done, f32[128]{0:T(128)S(1)} %fusion.40, bf16[128,2048]{1,0:T(8,128)(2,1)} %reduce-scatter.3.cloned.1.call-done, ...), kind=kOutput, calls=%fused_computation.35 | convolution fusion | flops 2015887360 | bytes 5046784 | tf_op jit(solution)/shard_map/dot_general | solution.py:210
  (85 shorter events, 10.7 us)
Async XLA Ops:
  6.5 41.4 %copy-start = (bf16[3,2048,256]{2,1,0:T(8,128)(2,1)S(1)}, bf16[3,2048,256]{2,1,0:T(8,128)(2,1)}, u32[]{:S(2)}) copy-start(bf16[3,2048,256]{2,1,0:T(8,128)(2,1)} %param.21) | copy-start | bytes 9437188
  6.5 38.2 %all-gather.3.cloned.1.call-start = ((), (), s32[]{:S(2)}) async-start(), calls=%async_computation.4 | async-start | bytes 4718592 | tf_op jit(solution)/shard_map/all_gather | solution.py:116
  7.3 113.4 %reduce-scatter.3.cloned.1.call-start = ((), (), s32[]{:S(2)}) async-start(), calls=%async_computation.5 | async-start | bytes 4718592 | tf_op jit(solution)/shard_map/reduce_scatter | solution.py:141
  10.2 6.7 %copy-start.19 = (s32[1,16]{1,0:T(1,128)S(1)}, s32[1,16]{1,0:T(1,128)}, u32[]{:S(2)}) copy-start(s32[1,16]{1,0:T(1,128)} %param.18) | copy-start | bytes 196
  13.8 3.1 %copy-start.2 = (bf16[16,2,128,256]{3,2,1,0:T(8,128)(2,1)S(1)}, bf16[16,2,128,256]{3,2,1,0:T(8,128)(2,1)}, u32[]{:S(2)}) copy-start(bf16[16,2,128,256]{3,2,1,0:T(8,128)(2,1)} %gather_fusion) | copy-start | bytes 6291460
  44.7 3.4 %copy-start.6 = (bf16[1024,2048]{1,0:T(8,128)(2,1)S(1)}, bf16[1024,2048]{1,0:T(8,128)(2,1)}, u32[]{:S(2)}) copy-start(bf16[1024,2048]{1,0:T(8,128)(2,1)} %all-gather.3.cloned.1.call-done) | copy-start | bytes 12582916
  51.6 1.8 copy-start.3
  54.5 2.3 copy-start.11
  56.8 2.4 copy-start.9
  56.8 2.7 copy-start.4
  59.6 1.2 copy-start.8
  60.8 1.7 copy-start.7
  60.8 1.9 copy-start.10
  64.0 17.6 %copy-start.12 = (bf16[256,2048]{1,0:T(8,128)(2,1)S(1)}, bf16[256,2048]{1,0:T(8,128)(2,1)}, u32[]{:S(2)}) copy-start(bf16[256,2048]{1,0:T(8,128)(2,1)} %param.23) | copy-start | bytes 3145732
  85.8 0.7 copy-start.14
  85.8 34.8 %copy-start.5 = (bf16[128,2048]{1,0:T(8,128)(2,1)S(1)}, bf16[128,2048]{1,0:T(8,128)(2,1)}, u32[]{:S(2)}) copy-start(bf16[128,2048]{1,0:T(8,128)(2,1)} %param.16) | copy-start | bytes 1572868
  85.8 38.2 %copy-start.13 = (s32[128,4]{0,1:T(4,128)S(1)}, s32[128,4]{0,1:T(4,128)}, u32[]{:S(2)}) copy-start(s32[128,4]{0,1:T(4,128)} %param.25) | copy-start | bytes 6148
  85.8 106.5 %all-gather.5.cloned.1.call-start = ((), (), s32[]{:S(2)}) async-start(), calls=%async_computation.6 | async-start | bytes 4718592 | tf_op jit(solution)/shard_map/all_gather | solution.py:151
  124.0 148.8 %reduce-scatter.5.cloned.1.call-start = ((), (), s32[]{:S(2)}) async-start(), calls=%async_computation.7 | async-start | bytes 4718592 | tf_op jit(solution)/shard_map/reduce_scatter | solution.py:157
  191.3 15.9 %collective-permute-start = (bf16[640,2048]{1,0:T(8,128)(2,1)}, bf16[640,2048]{1,0:T(8,128)(2,1)}, u32[]{:S(2)}, u32[]{:S(2)}) collective-permute-start(bf16[640,2048]{1,0:T(8,128)(2,1)} %bitcast.130), channel_id=1, source_target_pairs={{0,1},{1,0},{2,3},{3,2},{4,5},{5,4},{6,7},{7,6},{8,9},{9,8},{10,11... | collective-permute-start | bytes 7864328 | tf_op jit(solution)/shard_map/ppermute | solution.py:183
  192.3 9.6 %copy-start.17 = (bf16[704,2048]{1,0:T(8,128)(2,1)S(1)}, bf16[704,2048]{1,0:T(8,128)(2,1)}, u32[]{:S(2)}) copy-start(bf16[704,2048]{1,0:T(8,128)(2,1)} %param.30) | copy-start | bytes 8650756
  207.2 7.6 %copy-start.18 = (bf16[1,704,2048]{2,1,0:T(8,128)(2,1)S(1)}, bf16[1,704,2048]{2,1,0:T(8,128)(2,1)}, u32[]{:S(2)}) copy-start(bf16[1,704,2048]{2,1,0:T(8,128)(2,1)} %param.28) | copy-start | bytes 8650756
  217.1 7.1 %collective-permute-start.1 = (bf16[640,2048]{1,0:T(8,128)(2,1)S(1)}, bf16[640,2048]{1,0:T(8,128)(2,1)S(1)}, u32[]{:S(2)}, u32[]{:S(2)}) collective-permute-start(bf16[640,2048]{1,0:T(8,128)(2,1)S(1)} %convolution_convert_fusion.2), channel_id=1, source_target_pairs={{0,1},{1,0},{2,3},{3,2},{4,5},{5,4},{6,7},{7,6},{8,9},{9,8},{10,11... | collective-permute-start | bytes 7864328 | tf_op jit(solution)/shard_map/ppermute | solution.py:194
  228.9 5.7 %copy-start.15 = (bf16[2048]{0:T(1024)(128)(2,1)S(1)}, bf16[2048]{0:T(1024)(128)(2,1)}, u32[]{:S(2)}) copy-start(bf16[2048]{0:T(1024)(128)(2,1)} %param.31) | copy-start | bytes 12292
  229.0 5.7 %copy-start.16 = (f32[128,4]{0,1:T(4,128)S(1)}, f32[128,4]{0,1:T(4,128)}, u32[]{:S(2)}) copy-start(f32[128,4]{0,1:T(4,128)} %param.26) | copy-start | bytes 6148
  229.0 43.9 %all-to-all-start.1 = ((bf16[64,10,16,128]{3,2,1,0:T(8,128)(2,1)}), bf16[64,10,16,128]{3,2,1,0:T(8,128)(2,1)}, u32[]{:S(2)}, u32[]{:S(2)}) async-start(bf16[64,10,16,128]{3,2,1,0:T(8,128)(2,1)} %bitcast.35), calls=%async_computation.3 | async-start | bytes 5242880 | tf_op jit(solution)/shard_map/all_to_all | solution.py:198
  234.7 42.6 %copy-start.1 = (bf16[3,2048,256]{2,1,0:T(8,128)(2,1)S(1)}, bf16[3,2048,256]{2,1,0:T(8,128)(2,1)}, u32[]{:S(2)}) copy-start(bf16[3,2048,256]{2,1,0:T(8,128)(2,1)} %param.21) | copy-start | bytes 9437188
Sparse Core Ops, SparseCore 0:
  9.0 35.6 all-gather.2
  86.0 34.6 reduce-scatter.2
  124.1 60.5 all-gather.4
  207.4 30.4 reduce-scatter.4

commit v2 on v1

--- a/solution.py
+++ b/solution.py
@@ -146,17 +146,6 @@
     ).astype(jnp.float32)
     resid = (hidden_in.astype(jnp.float32) + attn_own).astype(jnp.bfloat16)
     mixed = rms_scale(resid, mlp_gain)
-    inner = jnp.einsum(
-        "td,dcf->tcf",
-        lax.all_gather(mixed, HEAD, axis=0, tiled=True),
-        w_shared_in,
-        preferred_element_type=jnp.float32,
-    )
-    activated = (jax.nn.silu(inner[:, 0]) * inner[:, 1]).astype(jnp.bfloat16)
-    shared_part = jnp.dot(activated, w_shared_out, preferred_element_type=jnp.float32)
-    shared_own = lax.psum_scatter(
-        shared_part.astype(jnp.bfloat16), HEAD, scatter_dimension=0, tiled=True
-    ).astype(jnp.float32)
     gate = jax.nn.sigmoid(jnp.dot(mixed, shared_gate, preferred_element_type=jnp.float32))
     flat_ids = expert_ids.reshape(-1)
     one_hot = (flat_ids[:, None] == jnp.arange(expert_count, dtype=jnp.int32)[None, :]).astype(
@@ -181,6 +170,8 @@
         expert_count * capacity, width
     )
     sibling = lax.ppermute(arrived, "core", pair)
+    arrived, mixed_late = lax.optimization_barrier((arrived, mixed))
+    mixed_all = lax.all_gather(mixed_late, HEAD, axis=0, tiled=True)
 
     def half_expert(rows):
         inner = jnp.dot(rows, w_experts_in[0], preferred_element_type=jnp.float32)
@@ -195,6 +186,18 @@
     merged_own = (part_own.astype(jnp.float32) + part_back.astype(jnp.float32)).astype(
         jnp.bfloat16
     )
+    _, mixed_all = lax.optimization_barrier((merged_own, mixed_all))
+    inner = jnp.einsum(
+        "td,dcf->tcf",
+        mixed_all,
+        w_shared_in,
+        preferred_element_type=jnp.float32,
+    )
+    activated = (jax.nn.silu(inner[:, 0]) * inner[:, 1]).astype(jnp.bfloat16)
+    shared_part = jnp.dot(activated, w_shared_out, preferred_element_type=jnp.float32)
+    shared_own = lax.psum_scatter(
+        shared_part.astype(jnp.bfloat16), HEAD, scatter_dimension=0, tiled=True
+    ).astype(jnp.float32)
     merged = lax.all_to_all(merged_own.reshape(tiles), ("tok", "x"), 0, 0, tiled=True).reshape(
         expert_count * capacity, width
     )

time: 284 us -> 290 us (1.021)
  waiting for transfers between devices: 97.4 us -> 113 us
  blocking collectives: 60 us -> 46.1 us
  starting transfers between devices: 7.13 us -> 11.3 us
    all_to_all x1, blocking collectives: 60 us -> 46.1 us  [per_device(): lax.all_to_all(buffer.reshape(tiles), ('tok', 'x'), 0, 0, tiled=True)]
    all_to_all x1, waiting for transfers between devices: 36.5 us -> 46.7 us  [per_device(): lax.all_to_all(merged_own.reshape(tiles), ('tok', 'x'), 0, 0, tiled=True)]
    ppermute x1, waiting for transfers between devices: 0.01 us -> 4.79 us  [per_device(): sibling = lax.ppermute(arrived, 'core', pair)]
    all_to_all x1, starting transfers between devices: 5.69 us -> 9.07 us  [per_device(): lax.all_to_all(merged_own.reshape(tiles), ('tok', 'x'), 0, 0, tiled=True)]
    unnamed x45 -> x49, local copies, waits for them, and re-layouts: 7.65 us -> 7.67 us
  transfers between devices with their start and end apart: 7 -> 7, of which waited for: 3 -> 5; matrix products, arithmetic and copies ran while one was open for 20% -> 13% of each run, Pallas kernels for 0% -> 0%
where the time goes in v2:
time: 290 us; the launch traced here: 289 us
  waiting for transfers between devices  113 us (39%)
  matrix products  49.5 us (17%)
  blocking collectives  46.1 us (16%)
  other arithmetic  21.5 us (7%)
  Pallas kernels  17.6 us (6%)
  local copies, waits for them, and re-layouts  16 us (6%)
  between operations  14.2 us (5%)
  starting transfers between devices  11.3 us (4%)
    all_to_all x1, waiting for transfers between devices, per_device(): lax.all_to_all(merged_own.reshape(tiles), ('tok', 'x'), 0, 0, tiled=True)  46.7 us
    all_to_all x1, blocking collectives, per_device(): lax.all_to_all(buffer.reshape(tiles), ('tok', 'x'), 0, 0, tiled=True)  46.1 us
    reduce_scatter x1, waiting for transfers between devices, per_device(): lax.psum_scatter(jnp.dot(heads_out, out_weight, preferred_element_type=jn...  31.8 us
    all_gather x1, waiting for transfers between devices, per_device(): gathered = lax.all_gather(hidden_in, HEAD, axis=0, tiled=True)  26 us
    pallas_call x1, Pallas kernels, attend(): pl.pallas_call(kernel, out_shape=jax.ShapeDtypeStruct((row_count, width),...  17.6 us
    dot_general x2, matrix products, half_expert(): inner = jnp.dot(rows, w_experts_in[0], preferred_element_type=jnp.float32)  15.7 us
    dot_general x1, matrix products, per_device(): jnp.einsum('td,dcf->tcf', mixed_all, w_shared_in, preferred_element_type=...  9.58 us
    all_to_all x1, starting transfers between devices, per_device(): lax.all_to_all(merged_own.reshape(tiles), ('tok', 'x'), 0, 0, tiled=True)  9.07 us
  transfers between devices with their start and end apart: 7, of which 5 were waited for; matrix products, arithmetic and copies ran while one was open for 13% of the time, Pallas kernels for 0%

profile of v2, /device:TPU:1, one launch (start us, length us, event | category | flops | bytes accessed | tf_op | source)
XLA Modules:
  0.0 288.6 jit_solution(10446301145143893266)
XLA Ops:
  10.2 3.6 %gather_fusion = bf16[16,2,128,256]{3,2,1,0:T(8,128)(2,1)} fusion(bf16[2,16,128,256]{3,2,1,0:T(8,128)(2,1)} %param.19, s32[1024]{0:T(1024)S(1)} %pad_clamp_fusion), kind=kCustom, calls=%fused_computation | custom fusion | bytes 4194368 | tf_op jit(solution)/shard_map/jit(_take)/gather | solution.py:133
  14.0 2.9 fusion.51
  17.2 1.5 fusion.62
  18.7 26.0 %all-gather.3.cloned.1.call-done = bf16[1024,2048]{1,0:T(8,128)(2,1)} async-done(((bf16[128,2048]{1,0:T(8,128)(2,1)}), bf16[1024,2048]{1,0:T(8,128)(2,1)}) %all-gather.3.cloned.1.call-update) | async-done | bytes 4194320 | tf_op jit(solution)/shard_map/all_gather | solution.py:116
  44.7 3.2 %fusion = f32[1024]{0:T(1024)S(1)} fusion(bf16[1024,2048]{1,0:T(8,128)(2,1)} %all-gather.3.cloned.1.call-done), kind=kLoop, calls=%fused_computation.3 | loop fusion | flops 6290432 | bytes 4198400 | tf_op jit(solution)/shard_map/reduce_sum | solution.py:21
  48.1 3.5 %add_bitcast_fusion = f32[3,1024,256]{2,1,0:T(8,128)S(1)} fusion(bf16[3,2048,256]{2,1,0:T(8,128)(2,1)S(1)} %copy-done, bf16[1024,2048]{1,0:T(8,128)(2,1)S(1)} %copy-done.7, f32[2048]{0:T(1024)S(1)} %convert_element_type.107, f32[1024]{0:T(1024)S(1)} %add_rsqrt_fusion, f32[3,256]{1,0:T(4,128)S(1)} %convert_element_type.109), kind=kOutput, calls=%fused_computation.22 | convolution fusion | flops 3230400512 | bytes 10501120 | tf_op jit(solution)/shard_map/td,cdf->ctf/dot_general | solution.py:121
  54.5 2.3 slice_negate_fusion
  56.8 2.3 maximum_multiply_fusion.1
  60.8 1.3 pad_maximum_fusion.key_ref
  62.7 1.2 pad_maximum_fusion.1.value_ref
  63.9 17.6 %shard_map.154 = bf16[1024,256]{1,0:T(8,128)(2,1)} custom-call(s32[1]{0:T(128)} %copy.70.context_ref, bf16[1024,256]{1,0:T(8,128)(2,1)} %get-tuple-element.12.query_ref, bf16[3072,256]{1,0:T(8,128)(2,1)} %pad_maximum_fusion.key_ref, bf16[3072,256]{1,0:T(8,128)(2,1)} %pad_maximum_fusion.1.value_ref), custom_call_target="tpu_custom_call" | custom-call | tf_op jit(solution)/shard_map/pallas_call | solution.py:69
  81.5 4.2 %convolution_convert_fusion.1 = bf16[1024,2048]{1,0:T(8,128)(2,1)} fusion(bf16[1024,256]{1,0:T(8,128)(2,1)} %shard_map.154, bf16[256,2048]{1,0:T(8,128)(2,1)S(1)} %copy-done.13), kind=kOutput, calls=%fused_computation.18 | convolution fusion | flops 1075838976 | bytes 5767168 | tf_op jit(solution)/shard_map/dot_general | solution.py:142
  86.8 1.2 reduce-window.6
  88.8 31.8 %reduce-scatter.3.cloned.1.call-done = bf16[128,2048]{1,0:T(8,128)(2,1)} async-done(((bf16[1024,2048]{1,0:T(8,128)(2,1)}), bf16[128,2048]{1,0:T(8,128)(2,1)}) %reduce-scatter.3.cloned.1.call-update) | async-done | bytes 524304 | tf_op jit(solution)/shard_map/reduce_scatter | solution.py:141
  120.6 1.3 fusion.40
  121.9 1.3 fusion.42
  124.9 46.1 %all_to_all.10 = bf16[64,10,16,128]{3,2,1,0:T(8,128)(2,1)S(1)} all-to-all(bf16[64,10,16,128]{3,2,1,0:T(8,128)(2,1)S(1)} %bitcast.131), channel_id=1, replica_groups=mesh['tok'=16,'x'=4,'core'=2] {'tok','x'}, dimensions={0} | all-to-all | bytes 5242880 | tf_op jit(solution)/shard_map/all_to_all | solution.py:169
  170.9 2.2 copy.69
  173.1 1.6 collective-permute-start
  174.8 4.8 %collective-permute-done = bf16[640,2048]{1,0:T(8,128)(2,1)} collective-permute-done((bf16[640,2048]{1,0:T(8,128)(2,1)}, bf16[640,2048]{1,0:T(8,128)(2,1)}, u32[]{:S(2)}, u32[]{:S(2)}) %collective-permute-start) | collective-permute-done | bytes 2621472 | tf_op jit(solution)/shard_map/ppermute | solution.py:172
  179.6 7.9 %fusion.3 = f32[640,1408]{1,0:T(8,128)S(1)} fusion(bf16[640,2048]{1,0:T(8,128)(2,1)} %collective-permute-done, bf16[1,2048,1408]{2,1,0:T(8,128)(2,1)} %param.27), kind=kOutput, calls=%fused_computation.6 | convolution fusion | flops 3690987520 | bytes 11993088 | tf_op jit(solution)/shard_map/dot_general | solution.py:177
  187.5 2.3 convolution_convert_fusion.2
  190.2 7.8 %fusion.5 = f32[640,1408]{1,0:T(8,128)S(1)} fusion(bf16[640,2048]{1,0:T(8,128)(2,1)} %bitcast.129, bf16[1,2048,1408]{2,1,0:T(8,128)(2,1)} %param.27), kind=kOutput, calls=%fused_computation.8 | convolution fusion | flops 3690987520 | bytes 11993088 | tf_op jit(solution)/shard_map/dot_general | solution.py:177
  198.1 2.3 add_convert_fusion
  200.4 2.5 all-gather.5.cloned.1.call-done
  202.9 9.6 %fusion.10 = f32[1024,2,704]{0,2,1:T(8,128)S(1)} fusion(bf16[2048,2,704]{0,2,1:T(8,128)(2,1)} %param.29, bf16[1024,2048]{1,0:T(8,128)(2,1)} %all-gather.5.cloned.1.call-done), kind=kOutput, calls=%fused_computation.13 | convolution fusion | flops 5905580032 | bytes 15728640 | tf_op jit(solution)/shard_map/td,dcf->tcf/dot_general | solution.py:190
  212.5 5.3 %convolution_convert_fusion = bf16[1024,2048]{1,0:T(8,128)(2,1)} fusion(bf16[704,2048]{1,0:T(8,128)(2,1)S(1)} %copy-done.20, f32[1024,2,704]{0,2,1:T(8,128)S(1)} %fusion.10), kind=kOutput, calls=%fused_computation.17 | convolution fusion | flops 2959212544 | bytes 12845056 | tf_op jit(solution)/shard_map/dot_general | solution.py:197
  217.8 2.4 copy.53
  220.2 9.1 %all-to-all-start.1 = ((bf16[64,10,16,128]{3,2,1,0:T(8,128)(2,1)}), bf16[64,10,16,128]{3,2,1,0:T(8,128)(2,1)}, u32[]{:S(2)}, u32[]{:S(2)}) async-start(bf16[64,10,16,128]{3,2,1,0:T(8,128)(2,1)} %bitcast.35), calls=%async_computation.3 | async-start | bytes 5242880 | tf_op jit(solution)/shard_map/all_to_all | solution.py:201
  229.5 1.4 fusion.39
  230.9 46.7 %all-to-all-done.1 = bf16[64,10,16,128]{3,2,1,0:T(8,128)(2,1)} async-done(((bf16[64,10,16,128]{3,2,1,0:T(8,128)(2,1)}), bf16[64,10,16,128]{3,2,1,0:T(8,128)(2,1)}, u32[]{:S(2)}, u32[]{:S(2)}) %all-to-all-start.1) | async-done | bytes 2621472 | tf_op jit(solution)/shard_map/all_to_all | solution.py:201
  277.6 4.5 %fusion.26 = bf16[128,2048]{1,0:T(8,128)(2,1)} fusion(f32[128,640]{1,0:T(8,128)S(1)} %select_reduce_fusion, bf16[80,8,16,128]{3,2,1,0:T(8,128)(2,1)} %bitcast.37, bf16[128,2048]{1,0:T(8,128)(2,1)} %reduce-scatter.5.cloned.1.call-done, f32[128]{0:T(128)S(1)} %fusion.39, bf16[128,2048]{1,0:T(8,128)(2,1)} %reduce-scatter.3.cloned.1.call-done, ...), kind=kOutput, calls=%fused_computation.34 | convolution fusion | flops 2015887360 | bytes 5046784 | tf_op jit(solution)/shard_map/dot_general | solution.py:213
  (89 shorter events, 13.0 us)
Async XLA Ops:
  6.5 41.4 %copy-start = (bf16[3,2048,256]{2,1,0:T(8,128)(2,1)S(1)}, bf16[3,2048,256]{2,1,0:T(8,128)(2,1)}, u32[]{:S(2)}) copy-start(bf16[3,2048,256]{2,1,0:T(8,128)(2,1)} %param.21) | copy-start | bytes 9437188
  6.5 38.2 %all-gather.3.cloned.1.call-start = ((), (), s32[]{:S(2)}) async-start(), calls=%async_computation.4 | async-start | bytes 4718592 | tf_op jit(solution)/shard_map/all_gather | solution.py:116
  7.3 113.3 %reduce-scatter.3.cloned.1.call-start = ((), (), s32[]{:S(2)}) async-start(), calls=%async_computation.5 | async-start | bytes 4718592 | tf_op jit(solution)/shard_map/reduce_scatter | solution.py:141
  10.2 6.7 %copy-start.21 = (s32[1,16]{1,0:T(1,128)S(1)}, s32[1,16]{1,0:T(1,128)}, u32[]{:S(2)}) copy-start(s32[1,16]{1,0:T(1,128)} %param.18) | copy-start | bytes 196
  13.8 3.1 %copy-start.2 = (bf16[16,2,128,256]{3,2,1,0:T(8,128)(2,1)S(1)}, bf16[16,2,128,256]{3,2,1,0:T(8,128)(2,1)}, u32[]{:S(2)}) copy-start(bf16[16,2,128,256]{3,2,1,0:T(8,128)(2,1)} %gather_fusion) | copy-start | bytes 6291460
  44.7 3.4 %copy-start.7 = (bf16[1024,2048]{1,0:T(8,128)(2,1)S(1)}, bf16[1024,2048]{1,0:T(8,128)(2,1)}, u32[]{:S(2)}) copy-start(bf16[1024,2048]{1,0:T(8,128)(2,1)} %all-gather.3.cloned.1.call-done) | copy-start | bytes 12582916
  51.6 1.8 copy-start.4
  54.5 2.3 copy-start.12
  56.8 2.4 copy-start.10
  56.8 2.7 copy-start.5
  59.6 1.2 copy-start.9
  60.8 1.7 copy-start.8
  60.8 1.9 copy-start.11
  63.9 17.6 %copy-start.13 = (bf16[256,2048]{1,0:T(8,128)(2,1)S(1)}, bf16[256,2048]{1,0:T(8,128)(2,1)}, u32[]{:S(2)}) copy-start(bf16[256,2048]{1,0:T(8,128)(2,1)} %param.23) | copy-start | bytes 3145732
  85.8 0.7 copy-start.14
  85.8 1.0 copy-start.15
  85.8 34.8 %copy-start.6 = (bf16[128,2048]{1,0:T(8,128)(2,1)S(1)}, bf16[128,2048]{1,0:T(8,128)(2,1)}, u32[]{:S(2)}) copy-start(bf16[128,2048]{1,0:T(8,128)(2,1)} %param.16) | copy-start | bytes 1572868
  85.8 117.0 %all-gather.5.cloned.1.call-start = ((), (), s32[]{:S(2)}) async-start(), calls=%async_computation.6 | async-start | bytes 4718592 | tf_op jit(solution)/shard_map/all_gather | solution.py:174
  123.2 1.7 copy-start.3
  173.1 6.5 %collective-permute-start = (bf16[640,2048]{1,0:T(8,128)(2,1)}, bf16[640,2048]{1,0:T(8,128)(2,1)}, u32[]{:S(2)}, u32[]{:S(2)}) collective-permute-start(bf16[640,2048]{1,0:T(8,128)(2,1)} %bitcast.129), channel_id=1, source_target_pairs={{0,1},{1,0},{2,3},{3,2},{4,5},{5,4},{6,7},{7,6},{8,9},{9,8},{10,11... | collective-permute-start | bytes 7864328 | tf_op jit(solution)/shard_map/ppermute | solution.py:172
  174.7 12.7 %copy-start.18 = (bf16[1,704,2048]{2,1,0:T(8,128)(2,1)S(1)}, bf16[1,704,2048]{2,1,0:T(8,128)(2,1)}, u32[]{:S(2)}) copy-start(bf16[1,704,2048]{2,1,0:T(8,128)(2,1)} %param.28) | copy-start | bytes 8650756
  174.8 102.9 %reduce-scatter.5.cloned.1.call-start = ((), (), s32[]{:S(2)}) async-start(), calls=%async_computation.7 | async-start | bytes 4718592 | tf_op jit(solution)/shard_map/reduce_scatter | solution.py:198
  189.8 8.3 %copy-start.19 = (bf16[1,704,2048]{2,1,0:T(8,128)(2,1)S(1)}, bf16[1,704,2048]{2,1,0:T(8,128)(2,1)}, u32[]{:S(2)}) copy-start(bf16[1,704,2048]{2,1,0:T(8,128)(2,1)} %param.28) | copy-start | bytes 8650756
  189.8 8.3 %collective-permute-start.1 = (bf16[640,2048]{1,0:T(8,128)(2,1)S(1)}, bf16[640,2048]{1,0:T(8,128)(2,1)S(1)}, u32[]{:S(2)}, u32[]{:S(2)}) collective-permute-start(bf16[640,2048]{1,0:T(8,128)(2,1)S(1)} %convolution_convert_fusion.2), channel_id=1, source_target_pairs={{0,1},{1,0},{2,3},{3,2},{4,5},{5,4},{6,7},{7,6},{8,9},{9,8},{10,11... | collective-permute-start | bytes 7864328 | tf_op jit(solution)/shard_map/ppermute | solution.py:185
  202.9 9.6 %copy-start.20 = (bf16[704,2048]{1,0:T(8,128)(2,1)S(1)}, bf16[704,2048]{1,0:T(8,128)(2,1)}, u32[]{:S(2)}) copy-start(bf16[704,2048]{1,0:T(8,128)(2,1)} %param.30) | copy-start | bytes 8650756
  220.2 9.1 %copy-start.16 = (bf16[2048]{0:T(1024)(128)(2,1)S(1)}, bf16[2048]{0:T(1024)(128)(2,1)}, u32[]{:S(2)}) copy-start(bf16[2048]{0:T(1024)(128)(2,1)} %param.31) | copy-start | bytes 12292
  220.2 9.1 %copy-start.17 = (f32[128,4]{0,1:T(4,128)S(1)}, f32[128,4]{0,1:T(4,128)}, u32[]{:S(2)}) copy-start(f32[128,4]{0,1:T(4,128)} %param.26) | copy-start | bytes 6148
  220.2 57.5 %all-to-all-start.1 = ((bf16[64,10,16,128]{3,2,1,0:T(8,128)(2,1)}), bf16[64,10,16,128]{3,2,1,0:T(8,128)(2,1)}, u32[]{:S(2)}, u32[]{:S(2)}) async-start(bf16[64,10,16,128]{3,2,1,0:T(8,128)(2,1)} %bitcast.35), calls=%async_computation.3 | async-start | bytes 5242880 | tf_op jit(solution)/shard_map/all_to_all | solution.py:201
  229.3 52.8 %copy-start.1 = (bf16[3,2048,256]{2,1,0:T(8,128)(2,1)S(1)}, bf16[3,2048,256]{2,1,0:T(8,128)(2,1)}, u32[]{:S(2)}) copy-start(bf16[3,2048,256]{2,1,0:T(8,128)(2,1)} %param.21) | copy-start | bytes 9437188
Sparse Core Ops, SparseCore 0:
  9.0 35.6 all-gather.2
  85.9 34.6 reduce-scatter.2
  174.9 27.9 all-gather.4
  217.9 59.6 reduce-scatter.4

commit v3 on v1

--- a/solution.py
+++ b/solution.py
@@ -113,10 +113,9 @@
     expert_count = device_count // 2
     top_count = expert_ids.shape[1]
     capacity = 2 * max(1, tok_rows * top_count * 5 // (8 * expert_count))
-    gathered = lax.all_gather(hidden_in, HEAD, axis=0, tiled=True)
-    stretch_rows = gathered.shape[0]
+    normed = lax.all_gather(rms_scale(hidden_in, attn_gain), HEAD, axis=0, tiled=True)
+    stretch_rows = normed.shape[0]
     heads_here = proj_weight.shape[2] // HD
-    normed = rms_scale(gathered, attn_gain)
     projected = (
         jnp.einsum("td,cdf->ctf", normed, proj_weight, preferred_element_type=jnp.float32)
         + proj_bias.astype(jnp.float32)[:, None, :]

time: 284 us -> 284 us (level)
    unnamed x45 -> x43, local copies, waits for them, and re-layouts: 7.65 us -> 7.29 us
  transfers between devices with their start and end apart: 7 -> 7, of which waited for: 3 -> 3; matrix products, arithmetic and copies ran while one was open for 20% -> 19% of each run, Pallas kernels for 0% -> 0%
where the time goes in v3:
time: 284 us; the launch traced here: 283 us
  waiting for transfers between devices  95.3 us (34%)
  blocking collectives  60.1 us (21%)
  matrix products  51 us (18%)
  other arithmetic  22.4 us (8%)
  Pallas kernels  17.6 us (6%)
  local copies, waits for them, and re-layouts  15.6 us (5%)
  between operations  14.1 us (5%)
  starting transfers between devices  7.29 us (3%)
    all_to_all x1, blocking collectives, per_device(): lax.all_to_all(buffer.reshape(tiles), ('tok', 'x'), 0, 0, tiled=True)  60.1 us
    all_to_all x1, waiting for transfers between devices, per_device(): lax.all_to_all(merged_own.reshape(tiles), ('tok', 'x'), 0, 0, tiled=True)  35.9 us
    reduce_scatter x1, waiting for transfers between devices, per_device(): lax.psum_scatter(jnp.dot(heads_out, out_weight, preferred_element_type=jn...  34.1 us
    all_gather x1, waiting for transfers between devices, per_device(): lax.all_gather(rms_scale(hidden_in, attn_gain), HEAD, axis=0, tiled=True)  25.2 us
    pallas_call x1, Pallas kernels, attend(): pl.pallas_call(kernel, out_shape=jax.ShapeDtypeStruct((row_count, width),...  17.6 us
    dot_general x2, matrix products, half_expert(): inner = jnp.dot(rows, w_experts_in[0], preferred_element_type=jnp.float32)  14.2 us
    dot_general x1, matrix products, per_device(): jnp.einsum('td,dcf->tcf', lax.all_gather(mixed, HEAD, axis=0, tiled=True)...  9.58 us
    unnamed x43, local copies, waits for them, and re-layouts  7.29 us
  transfers between devices with their start and end apart: 7, of which 3 were waited for; matrix products, arithmetic and copies ran while one was open for 19% of the time, Pallas kernels for 0%

profile of v3, /device:TPU:1, one launch (start us, length us, event | category | flops | bytes accessed | tf_op | source)
XLA Modules:
  0.0 283.4 jit_solution(12423226247034357328)
XLA Ops:
  7.4 1.3 fusion.35
  8.7 2.0 fusion.37
  12.8 3.6 %gather_fusion = bf16[16,2,128,256]{3,2,1,0:T(8,128)(2,1)} fusion(bf16[2,16,128,256]{3,2,1,0:T(8,128)(2,1)} %param.19, s32[1024]{0:T(1024)S(1)} %pad_clamp_fusion), kind=kCustom, calls=%fused_computation | custom fusion | bytes 4194368 | tf_op jit(solution)/shard_map/jit(_take)/gather | solution.py:132
  16.7 2.9 %fusion.50 = (f32[1024,128]{1,0:T(8,128)}, f32[1024,128]{1,0:T(8,128)}) fusion(f32[1024,64]{1,0:T(8,128)S(1)} %broadcast_multiply_fusion), kind=kLoop, calls=%fused_computation.76 | loop fusion | flops 131072 | bytes 1310720 | tf_op jit(solution)/shard_map/cos | solution.py:31
  19.9 1.5 fusion.61
  21.3 25.2 %all-gather.3.cloned.1.call-done = bf16[1024,2048]{1,0:T(8,128)(2,1)} async-done(((bf16[128,2048]{1,0:T(8,128)(2,1)}), bf16[1024,2048]{1,0:T(8,128)(2,1)}) %all-gather.3.cloned.1.call-update) | async-done | bytes 4194320 | tf_op jit(solution)/shard_map/all_gather | solution.py:116
  46.6 5.2 %add_bitcast_fusion = f32[3,1024,256]{2,1,0:T(8,128)S(1)} fusion(bf16[3,2048,256]{2,1,0:T(8,128)(2,1)S(1)} %copy-done, bf16[1024,2048]{1,0:T(8,128)(2,1)} %all-gather.3.cloned.1.call-done, f32[3,256]{1,0:T(4,128)S(1)} %convert_element_type.106), kind=kOutput, calls=%fused_computation.15 | convolution fusion | flops 3222011904 | bytes 10488832 | tf_op jit(solution)/shard_map/td,cdf->ctf/dot_general | solution.py:120
  54.6 2.3 slice_negate_fusion
  57.0 2.3 maximum_multiply_fusion.1
  59.7 1.2 fusion.42
  60.9 1.3 pad_maximum_fusion.key_ref
  62.9 1.3 pad_maximum_fusion.1.value_ref
  64.1 17.6 %shard_map.154 = bf16[1024,256]{1,0:T(8,128)(2,1)} custom-call(s32[1]{0:T(128)} %copy.71.context_ref, bf16[1024,256]{1,0:T(8,128)(2,1)} %get-tuple-element.6.query_ref, bf16[3072,256]{1,0:T(8,128)(2,1)} %pad_maximum_fusion.key_ref, bf16[3072,256]{1,0:T(8,128)(2,1)} %pad_maximum_fusion.1.value_ref), custom_call_target="tpu_custom_call" | custom-call | tf_op jit(solution)/shard_map/pallas_call | solution.py:69
  81.7 4.3 %convolution_convert_fusion.1 = bf16[1024,2048]{1,0:T(8,128)(2,1)} fusion(bf16[1024,256]{1,0:T(8,128)(2,1)} %shard_map.154, bf16[256,2048]{1,0:T(8,128)(2,1)S(1)} %copy-done.11), kind=kOutput, calls=%fused_computation.11 | convolution fusion | flops 1075838976 | bytes 5767168 | tf_op jit(solution)/shard_map/dot_general | solution.py:141
  86.7 34.1 %reduce-scatter.3.cloned.1.call-done = bf16[128,2048]{1,0:T(8,128)(2,1)} async-done(((bf16[1024,2048]{1,0:T(8,128)(2,1)}), bf16[128,2048]{1,0:T(8,128)(2,1)}) %reduce-scatter.3.cloned.1.call-update) | async-done | bytes 524304 | tf_op jit(solution)/shard_map/reduce_scatter | solution.py:140
  120.7 1.3 fusion.39
  122.0 2.0 fusion.41
  124.5 1.2 reduce-window.6
  126.5 1.9 fusion.26
  129.2 60.1 %all_to_all.10 = bf16[64,10,16,128]{3,2,1,0:T(8,128)(2,1)S(1)} all-to-all(bf16[64,10,16,128]{3,2,1,0:T(8,128)(2,1)S(1)} %bitcast.134), channel_id=1, replica_groups=mesh['tok'=16,'x'=4,'core'=2] {'tok','x'}, dimensions={0} | all-to-all | bytes 5242880 | tf_op jit(solution)/shard_map/all_to_all | solution.py:179
  189.3 2.2 copy.70
  192.5 9.6 %fusion.4 = f32[1024,2,704]{0,2,1:T(8,128)S(1)} fusion(bf16[2048,2,704]{0,2,1:T(8,128)(2,1)} %param.29, bf16[1024,2048]{1,0:T(8,128)(2,1)} %all-gather.5.cloned.1.call-done), kind=kOutput, calls=%fused_computation.6 | convolution fusion | flops 5905580032 | bytes 15728640 | tf_op jit(solution)/shard_map/td,dcf->tcf/dot_general | solution.py:148
  202.1 5.3 %convolution_convert_fusion = bf16[1024,2048]{1,0:T(8,128)(2,1)} fusion(bf16[704,2048]{1,0:T(8,128)(2,1)S(1)} %copy-done.16, f32[1024,2,704]{0,2,1:T(8,128)S(1)} %fusion.4), kind=kOutput, calls=%fused_computation.10 | convolution fusion | flops 2959212544 | bytes 12845056 | tf_op jit(solution)/shard_map/dot_general | solution.py:155
  207.4 7.5 %fusion = f32[640,1408]{1,0:T(8,128)S(1)} fusion(bf16[640,2048]{1,0:T(8,128)(2,1)} %collective-permute-done, bf16[1,2048,1408]{2,1,0:T(8,128)(2,1)} %param.27), kind=kOutput, calls=%fused_computation.1 | convolution fusion | flops 3690987520 | bytes 11993088 | tf_op jit(solution)/shard_map/dot_general | solution.py:185
  215.0 2.3 convolution_convert_fusion.2
  217.6 6.7 %fusion.2 = f32[640,1408]{1,0:T(8,128)S(1)} fusion(bf16[1,2048,1408]{2,1,0:T(8,128)(2,1)} %param.27, bf16[80,8,16,128]{3,2,1,0:T(8,128)(2,1)S(1)} %bitcast.133), kind=kOutput, calls=%fused_computation.3 | convolution fusion | flops 3690987520 | bytes 11993088 | tf_op jit(solution)/shard_map/dot_general | solution.py:185
  224.3 2.4 fusion.12
  226.7 2.4 copy.53
  229.1 5.7 %all-to-all-start.1 = ((bf16[64,10,16,128]{3,2,1,0:T(8,128)(2,1)}), bf16[64,10,16,128]{3,2,1,0:T(8,128)(2,1)}, u32[]{:S(2)}, u32[]{:S(2)}) async-start(bf16[64,10,16,128]{3,2,1,0:T(8,128)(2,1)} %bitcast.35), calls=%async_computation.3 | async-start | bytes 5242880 | tf_op jit(solution)/shard_map/all_to_all | solution.py:197
  235.1 1.4 fusion.34
  236.5 35.9 %all-to-all-done.1 = bf16[64,10,16,128]{3,2,1,0:T(8,128)(2,1)} async-done(((bf16[64,10,16,128]{3,2,1,0:T(8,128)(2,1)}), bf16[64,10,16,128]{3,2,1,0:T(8,128)(2,1)}, u32[]{:S(2)}, u32[]{:S(2)}) %all-to-all-start.1) | async-done | bytes 2621472 | tf_op jit(solution)/shard_map/all_to_all | solution.py:197
  272.5 4.5 %fusion.21 = bf16[128,2048]{1,0:T(8,128)(2,1)} fusion(f32[128,640]{1,0:T(8,128)S(1)} %select_reduce_fusion, bf16[80,8,16,128]{3,2,1,0:T(8,128)(2,1)} %bitcast.37, bf16[128,2048]{1,0:T(8,128)(2,1)} %reduce-scatter.5.cloned.1.call-done, f32[128]{0:T(128)S(1)} %fusion.34, bf16[128,2048]{1,0:T(8,128)(2,1)} %reduce-scatter.3.cloned.1.call-done, ...), kind=kOutput, calls=%fused_computation.28 | convolution fusion | flops 2015887360 | bytes 5046784 | tf_op jit(solution)/shard_map/dot_general | solution.py:209
  (84 shorter events, 10.9 us)
Async XLA Ops:
  6.5 40.0 %copy-start = (bf16[3,2048,256]{2,1,0:T(8,128)(2,1)S(1)}, bf16[3,2048,256]{2,1,0:T(8,128)(2,1)}, u32[]{:S(2)}) copy-start(bf16[3,2048,256]{2,1,0:T(8,128)(2,1)} %param.21) | copy-start | bytes 9437188
  6.5 40.0 %all-gather.3.cloned.1.call-start = ((), (), s32[]{:S(2)}) async-start(), calls=%async_computation.4 | async-start | bytes 4718592 | tf_op jit(solution)/shard_map/all_gather | solution.py:116
  10.8 110.0 %reduce-scatter.3.cloned.1.call-start = ((), (), s32[]{:S(2)}) async-start(), calls=%async_computation.5 | async-start | bytes 4718592 | tf_op jit(solution)/shard_map/reduce_scatter | solution.py:140
  12.8 6.7 %copy-start.18 = (s32[1,16]{1,0:T(1,128)S(1)}, s32[1,16]{1,0:T(1,128)}, u32[]{:S(2)}) copy-start(s32[1,16]{1,0:T(1,128)} %param.18) | copy-start | bytes 196
  16.5 3.1 %copy-start.2 = (bf16[16,2,128,256]{3,2,1,0:T(8,128)(2,1)S(1)}, bf16[16,2,128,256]{3,2,1,0:T(8,128)(2,1)}, u32[]{:S(2)}) copy-start(bf16[16,2,128,256]{3,2,1,0:T(8,128)(2,1)} %gather_fusion) | copy-start | bytes 6291460
  51.8 1.8 copy-start.4
  54.6 2.3 copy-start.10
  57.0 2.4 copy-start.8
  57.0 2.7 copy-start.5
  59.7 1.2 copy-start.7
  60.9 1.7 copy-start.6
  60.9 1.9 copy-start.9
  64.1 17.6 %copy-start.11 = (bf16[256,2048]{1,0:T(8,128)(2,1)S(1)}, bf16[256,2048]{1,0:T(8,128)(2,1)}, u32[]{:S(2)}) copy-start(bf16[256,2048]{1,0:T(8,128)(2,1)} %param.23) | copy-start | bytes 3145732
  86.0 0.7 copy-start.13
  86.0 34.8 %copy-start.3 = (bf16[128,2048]{1,0:T(8,128)(2,1)S(1)}, bf16[128,2048]{1,0:T(8,128)(2,1)}, u32[]{:S(2)}) copy-start(bf16[128,2048]{1,0:T(8,128)(2,1)} %param.16) | copy-start | bytes 1572868
  86.0 38.2 %copy-start.12 = (s32[128,4]{0,1:T(4,128)S(1)}, s32[128,4]{0,1:T(4,128)}, u32[]{:S(2)}) copy-start(s32[128,4]{0,1:T(4,128)} %param.25) | copy-start | bytes 6148
  86.0 106.5 %all-gather.5.cloned.1.call-start = ((), (), s32[]{:S(2)}) async-start(), calls=%async_computation.6 | async-start | bytes 4718592 | tf_op jit(solution)/shard_map/all_gather | solution.py:150
  124.1 148.3 %reduce-scatter.5.cloned.1.call-start = ((), (), s32[]{:S(2)}) async-start(), calls=%async_computation.7 | async-start | bytes 4718592 | tf_op jit(solution)/shard_map/reduce_scatter | solution.py:156
  191.5 15.9 %collective-permute-start = (bf16[640,2048]{1,0:T(8,128)(2,1)}, bf16[640,2048]{1,0:T(8,128)(2,1)}, u32[]{:S(2)}, u32[]{:S(2)}) collective-permute-start(bf16[640,2048]{1,0:T(8,128)(2,1)} %bitcast.130), channel_id=1, source_target_pairs={{0,1},{1,0},{2,3},{3,2},{4,5},{5,4},{6,7},{7,6},{8,9},{9,8},{10,11... | collective-permute-start | bytes 7864328 | tf_op jit(solution)/shard_map/ppermute | solution.py:182
  192.5 9.6 %copy-start.16 = (bf16[704,2048]{1,0:T(8,128)(2,1)S(1)}, bf16[704,2048]{1,0:T(8,128)(2,1)}, u32[]{:S(2)}) copy-start(bf16[704,2048]{1,0:T(8,128)(2,1)} %param.30) | copy-start | bytes 8650756
  207.4 7.6 %copy-start.17 = (bf16[1,704,2048]{2,1,0:T(8,128)(2,1)S(1)}, bf16[1,704,2048]{2,1,0:T(8,128)(2,1)}, u32[]{:S(2)}) copy-start(bf16[1,704,2048]{2,1,0:T(8,128)(2,1)} %param.28) | copy-start | bytes 8650756
  217.3 7.0 %collective-permute-start.1 = (bf16[640,2048]{1,0:T(8,128)(2,1)S(1)}, bf16[640,2048]{1,0:T(8,128)(2,1)S(1)}, u32[]{:S(2)}, u32[]{:S(2)}) collective-permute-start(bf16[640,2048]{1,0:T(8,128)(2,1)S(1)} %convolution_convert_fusion.2), channel_id=1, source_target_pairs={{0,1},{1,0},{2,3},{3,2},{4,5},{5,4},{6,7},{7,6},{8,9},{9,8},{10,11... | collective-permute-start | bytes 7864328 | tf_op jit(solution)/shard_map/ppermute | solution.py:193
  229.1 5.7 %copy-start.14 = (bf16[2048]{0:T(1024)(128)(2,1)S(1)}, bf16[2048]{0:T(1024)(128)(2,1)}, u32[]{:S(2)}) copy-start(bf16[2048]{0:T(1024)(128)(2,1)} %param.31) | copy-start | bytes 12292
  229.1 5.7 %copy-start.15 = (f32[128,4]{0,1:T(4,128)S(1)}, f32[128,4]{0,1:T(4,128)}, u32[]{:S(2)}) copy-start(f32[128,4]{0,1:T(4,128)} %param.26) | copy-start | bytes 6148
  229.1 43.3 %all-to-all-start.1 = ((bf16[64,10,16,128]{3,2,1,0:T(8,128)(2,1)}), bf16[64,10,16,128]{3,2,1,0:T(8,128)(2,1)}, u32[]{:S(2)}, u32[]{:S(2)}) async-start(bf16[64,10,16,128]{3,2,1,0:T(8,128)(2,1)} %bitcast.35), calls=%async_computation.3 | async-start | bytes 5242880 | tf_op jit(solution)/shard_map/all_to_all | solution.py:197
  234.8 42.1 %copy-start.1 = (bf16[3,2048,256]{2,1,0:T(8,128)(2,1)S(1)}, bf16[3,2048,256]{2,1,0:T(8,128)(2,1)}, u32[]{:S(2)}) copy-start(bf16[3,2048,256]{2,1,0:T(8,128)(2,1)} %param.21) | copy-start | bytes 9437188
Sparse Core Ops, SparseCore 0:
  10.9 35.6 all-gather.2
  86.1 34.5 reduce-scatter.2
  124.2 60.5 all-gather.4
  207.5 30.4 reduce-scatter.4

commit v4 on v3

--- a/solution.py
+++ b/solution.py
@@ -40,30 +40,46 @@
     scale = 1.0 / math.sqrt(head_size)
 
     def kernel(context_ref, query_ref, key_ref, value_ref, out_ref):
-        scores = (
+        query = query_ref[...]
+        dims = (((1,), (1,)), ((), ()))
+        cached_scores = (
             lax.dot_general(
-                query_ref[...],
-                key_ref[...],
-                (((1,), (1,)), ((), ())),
-                preferred_element_type=jnp.float32,
+                query, key_ref[:span_len, :], dims, preferred_element_type=jnp.float32
             )
             * scale
         )
-        key_pos = lax.broadcasted_iota(jnp.int32, scores.shape, 1)
+        new_scores = (
+            lax.dot_general(
+                query, key_ref[span_len:, :], dims, preferred_element_type=jnp.float32
+            )
+            * scale
+        )
+        cached_pos = lax.broadcasted_iota(jnp.int32, cached_scores.shape, 1)
+        cached_scores = jnp.where(cached_pos < context_ref[0], cached_scores, -1e30)
+        new_pos = lax.broadcasted_iota(jnp.int32, new_scores.shape, 1)
         query_pos = pl.program_id(1) * block_rows + lax.broadcasted_iota(
-            jnp.int32, scores.shape, 0
-        )
-        cached = key_pos < span_len
-        allowed = (cached & (key_pos < context_ref[0])) | (
-            jnp.logical_not(cached) & (key_pos - span_len <= query_pos)
-        )
-        scores = jnp.where(allowed, scores, -1e30)
-        largest = jnp.max(scores, axis=-1, keepdims=True)
-        weights = jnp.where(allowed, jnp.exp(scores - largest), 0.0)
-        probs = (weights / jnp.sum(weights, axis=-1, keepdims=True)).astype(jnp.bfloat16)
-        out_ref[...] = jnp.dot(probs, value_ref[...], preferred_element_type=jnp.float32).astype(
-            jnp.bfloat16
-        )
+            jnp.int32, new_scores.shape, 0
+        )
+        new_scores = jnp.where(new_pos <= query_pos, new_scores, -1e30)
+        largest = jnp.maximum(
+            jnp.max(cached_scores, axis=-1, keepdims=True),
+            jnp.max(new_scores, axis=-1, keepdims=True),
+        )
+        cached_weights = jnp.exp(cached_scores - largest)
+        new_weights = jnp.exp(new_scores - largest)
+        total = jnp.sum(cached_weights, axis=-1, keepdims=True) + jnp.sum(
+            new_weights, axis=-1, keepdims=True
+        )
+        out = jnp.dot(
+            (cached_weights / total).astype(jnp.bfloat16),
+            value_ref[:span_len, :],
+            preferred_element_type=jnp.float32,
+        ) + jnp.dot(
+            (new_weights / total).astype(jnp.bfloat16),
+            value_ref[span_len:, :],
+            preferred_element_type=jnp.float32,
+        )
+        out_ref[...] = out.astype(jnp.bfloat16)
 
     width = head_count * head_size
     result = pl.pallas_call(

time: 284 us -> 283 us (level)
  no operation moved by 1% of the time
where the time goes in v4:
time: 283 us; the launch traced here: 282 us
  waiting for transfers between devices  95.4 us (34%)
  blocking collectives  60.1 us (21%)
  matrix products  51 us (18%)
  other arithmetic  22.4 us (8%)
  Pallas kernels  16.6 us (6%)
  local copies, waits for them, and re-layouts  15.6 us (6%)
  between operations  14.1 us (5%)
  starting transfers between devices  7.29 us (3%)
    all_to_all x1, blocking collectives, per_device(): lax.all_to_all(buffer.reshape(tiles), ('tok', 'x'), 0, 0, tiled=True)  60.1 us
    all_to_all x1, waiting for transfers between devices, per_device(): lax.all_to_all(merged_own.reshape(tiles), ('tok', 'x'), 0, 0, tiled=True)  36 us
    reduce_scatter x1, waiting for transfers between devices, per_device(): lax.psum_scatter(jnp.dot(heads_out, out_weight, preferred_element_type=jn...  34.1 us
    all_gather x1, waiting for transfers between devices, per_device(): lax.all_gather(rms_scale(hidden_in, attn_gain), HEAD, axis=0, tiled=True)  25.2 us
    pallas_call x1, Pallas kernels, attend(): pl.pallas_call(kernel, out_shape=jax.ShapeDtypeStruct((row_count, width),...  16.6 us
    dot_general x2, matrix products, half_expert(): inner = jnp.dot(rows, w_experts_in[0], preferred_element_type=jnp.float32)  14.2 us
    dot_general x1, matrix products, per_device(): jnp.einsum('td,dcf->tcf', lax.all_gather(mixed, HEAD, axis=0, tiled=True)...  9.58 us
    unnamed x43, local copies, waits for them, and re-layouts  7.29 us
  transfers between devices with their start and end apart: 7, of which 3 were waited for; matrix products, arithmetic and copies ran while one was open for 19% of the time, Pallas kernels for 0%

profile of v4, /device:TPU:1, one launch (start us, length us, event | category | flops | bytes accessed | tf_op | source)
XLA Modules:
  0.0 282.5 jit_solution(12360558060024802479)
XLA Ops:
  7.4 1.3 fusion.35
  8.7 2.0 fusion.37
  12.8 3.6 %gather_fusion = bf16[16,2,128,256]{3,2,1,0:T(8,128)(2,1)} fusion(bf16[2,16,128,256]{3,2,1,0:T(8,128)(2,1)} %param.19, s32[1024]{0:T(1024)S(1)} %pad_clamp_fusion), kind=kCustom, calls=%fused_computation | custom fusion | bytes 4194368 | tf_op jit(solution)/shard_map/jit(_take)/gather | solution.py:148
  16.7 2.9 %fusion.50 = (f32[1024,128]{1,0:T(8,128)}, f32[1024,128]{1,0:T(8,128)}) fusion(f32[1024,64]{1,0:T(8,128)S(1)} %broadcast_multiply_fusion), kind=kLoop, calls=%fused_computation.76 | loop fusion | flops 131072 | bytes 1310720 | tf_op jit(solution)/shard_map/cos | solution.py:31
  19.9 1.5 fusion.61
  21.3 25.2 %all-gather.3.cloned.1.call-done = bf16[1024,2048]{1,0:T(8,128)(2,1)} async-done(((bf16[128,2048]{1,0:T(8,128)(2,1)}), bf16[1024,2048]{1,0:T(8,128)(2,1)}) %all-gather.3.cloned.1.call-update) | async-done | bytes 4194320 | tf_op jit(solution)/shard_map/all_gather | solution.py:132
  46.6 5.2 %add_bitcast_fusion = f32[3,1024,256]{2,1,0:T(8,128)S(1)} fusion(bf16[3,2048,256]{2,1,0:T(8,128)(2,1)S(1)} %copy-done, bf16[1024,2048]{1,0:T(8,128)(2,1)} %all-gather.3.cloned.1.call-done, f32[3,256]{1,0:T(4,128)S(1)} %convert_element_type.106), kind=kOutput, calls=%fused_computation.15 | convolution fusion | flops 3222011904 | bytes 10488832 | tf_op jit(solution)/shard_map/td,cdf->ctf/dot_general | solution.py:136
  54.6 2.3 slice_negate_fusion
  57.0 2.3 maximum_multiply_fusion.1
  59.7 1.2 fusion.42
  60.9 1.3 pad_maximum_fusion.key_ref
  62.9 1.3 pad_maximum_fusion.1.value_ref
  64.1 16.6 %shard_map.154 = bf16[1024,256]{1,0:T(8,128)(2,1)} custom-call(s32[1]{0:T(128)} %copy.71.context_ref, bf16[1024,256]{1,0:T(8,128)(2,1)} %get-tuple-element.6.query_ref, bf16[3072,256]{1,0:T(8,128)(2,1)} %pad_maximum_fusion.key_ref, bf16[3072,256]{1,0:T(8,128)(2,1)} %pad_maximum_fusion.1.value_ref), custom_call_target="tpu_custom_call" | custom-call | tf_op jit(solution)/shard_map/pallas_call | solution.py:85
  80.7 4.3 %convolution_convert_fusion.1 = bf16[1024,2048]{1,0:T(8,128)(2,1)} fusion(bf16[1024,256]{1,0:T(8,128)(2,1)} %shard_map.154, bf16[256,2048]{1,0:T(8,128)(2,1)S(1)} %copy-done.11), kind=kOutput, calls=%fused_computation.11 | convolution fusion | flops 1075838976 | bytes 5767168 | tf_op jit(solution)/shard_map/dot_general | solution.py:157
  85.6 34.1 %reduce-scatter.3.cloned.1.call-done = bf16[128,2048]{1,0:T(8,128)(2,1)} async-done(((bf16[1024,2048]{1,0:T(8,128)(2,1)}), bf16[128,2048]{1,0:T(8,128)(2,1)}) %reduce-scatter.3.cloned.1.call-update) | async-done | bytes 524304 | tf_op jit(solution)/shard_map/reduce_scatter | solution.py:156
  119.7 1.3 fusion.39
  121.0 2.0 fusion.41
  123.5 1.2 reduce-window.6
  125.5 1.9 fusion.26
  128.1 60.1 %all_to_all.10 = bf16[64,10,16,128]{3,2,1,0:T(8,128)(2,1)S(1)} all-to-all(bf16[64,10,16,128]{3,2,1,0:T(8,128)(2,1)S(1)} %bitcast.134), channel_id=1, replica_groups=mesh['tok'=16,'x'=4,'core'=2] {'tok','x'}, dimensions={0} | all-to-all | bytes 5242880 | tf_op jit(solution)/shard_map/all_to_all | solution.py:195
  188.3 2.2 copy.70
  191.5 9.6 %fusion.4 = f32[1024,2,704]{0,2,1:T(8,128)S(1)} fusion(bf16[2048,2,704]{0,2,1:T(8,128)(2,1)} %param.29, bf16[1024,2048]{1,0:T(8,128)(2,1)} %all-gather.5.cloned.1.call-done), kind=kOutput, calls=%fused_computation.6 | convolution fusion | flops 5905580032 | bytes 15728640 | tf_op jit(solution)/shard_map/td,dcf->tcf/dot_general | solution.py:164
  201.1 5.3 %convolution_convert_fusion = bf16[1024,2048]{1,0:T(8,128)(2,1)} fusion(bf16[704,2048]{1,0:T(8,128)(2,1)S(1)} %copy-done.16, f32[1024,2,704]{0,2,1:T(8,128)S(1)} %fusion.4), kind=kOutput, calls=%fused_computation.10 | convolution fusion | flops 2959212544 | bytes 12845056 | tf_op jit(solution)/shard_map/dot_general | solution.py:171
  206.4 7.5 %fusion = f32[640,1408]{1,0:T(8,128)S(1)} fusion(bf16[640,2048]{1,0:T(8,128)(2,1)} %collective-permute-done, bf16[1,2048,1408]{2,1,0:T(8,128)(2,1)} %param.27), kind=kOutput, calls=%fused_computation.1 | convolution fusion | flops 3690987520 | bytes 11993088 | tf_op jit(solution)/shard_map/dot_general | solution.py:201
  214.0 2.3 convolution_convert_fusion.2
  216.6 6.7 %fusion.2 = f32[640,1408]{1,0:T(8,128)S(1)} fusion(bf16[1,2048,1408]{2,1,0:T(8,128)(2,1)} %param.27, bf16[80,8,16,128]{3,2,1,0:T(8,128)(2,1)S(1)} %bitcast.133), kind=kOutput, calls=%fused_computation.3 | convolution fusion | flops 3690987520 | bytes 11993088 | tf_op jit(solution)/shard_map/dot_general | solution.py:201
  223.3 2.4 fusion.12
  225.7 2.4 copy.53
  228.1 5.7 %all-to-all-start.1 = ((bf16[64,10,16,128]{3,2,1,0:T(8,128)(2,1)}), bf16[64,10,16,128]{3,2,1,0:T(8,128)(2,1)}, u32[]{:S(2)}, u32[]{:S(2)}) async-start(bf16[64,10,16,128]{3,2,1,0:T(8,128)(2,1)} %bitcast.35), calls=%async_computation.3 | async-start | bytes 5242880 | tf_op jit(solution)/shard_map/all_to_all | solution.py:213
  234.0 1.4 fusion.34
  235.5 36.0 %all-to-all-done.1 = bf16[64,10,16,128]{3,2,1,0:T(8,128)(2,1)} async-done(((bf16[64,10,16,128]{3,2,1,0:T(8,128)(2,1)}), bf16[64,10,16,128]{3,2,1,0:T(8,128)(2,1)}, u32[]{:S(2)}, u32[]{:S(2)}) %all-to-all-start.1) | async-done | bytes 2621472 | tf_op jit(solution)/shard_map/all_to_all | solution.py:213
  271.5 4.5 %fusion.21 = bf16[128,2048]{1,0:T(8,128)(2,1)} fusion(f32[128,640]{1,0:T(8,128)S(1)} %select_reduce_fusion, bf16[80,8,16,128]{3,2,1,0:T(8,128)(2,1)} %bitcast.37, bf16[128,2048]{1,0:T(8,128)(2,1)} %reduce-scatter.5.cloned.1.call-done, f32[128]{0:T(128)S(1)} %fusion.34, bf16[128,2048]{1,0:T(8,128)(2,1)} %reduce-scatter.3.cloned.1.call-done, ...), kind=kOutput, calls=%fused_computation.28 | convolution fusion | flops 2015887360 | bytes 5046784 | tf_op jit(solution)/shard_map/dot_general | solution.py:225
  (84 shorter events, 10.9 us)
Async XLA Ops:
  6.5 40.0 %copy-start = (bf16[3,2048,256]{2,1,0:T(8,128)(2,1)S(1)}, bf16[3,2048,256]{2,1,0:T(8,128)(2,1)}, u32[]{:S(2)}) copy-start(bf16[3,2048,256]{2,1,0:T(8,128)(2,1)} %param.21) | copy-start | bytes 9437188
  6.5 40.0 %all-gather.3.cloned.1.call-start = ((), (), s32[]{:S(2)}) async-start(), calls=%async_computation.4 | async-start | bytes 4718592 | tf_op jit(solution)/shard_map/all_gather | solution.py:132
  10.8 108.9 %reduce-scatter.3.cloned.1.call-start = ((), (), s32[]{:S(2)}) async-start(), calls=%async_computation.5 | async-start | bytes 4718592 | tf_op jit(solution)/shard_map/reduce_scatter | solution.py:156
  12.8 6.7 %copy-start.18 = (s32[1,16]{1,0:T(1,128)S(1)}, s32[1,16]{1,0:T(1,128)}, u32[]{:S(2)}) copy-start(s32[1,16]{1,0:T(1,128)} %param.18) | copy-start | bytes 196
  16.5 3.1 %copy-start.2 = (bf16[16,2,128,256]{3,2,1,0:T(8,128)(2,1)S(1)}, bf16[16,2,128,256]{3,2,1,0:T(8,128)(2,1)}, u32[]{:S(2)}) copy-start(bf16[16,2,128,256]{3,2,1,0:T(8,128)(2,1)} %gather_fusion) | copy-start | bytes 6291460
  51.8 1.8 copy-start.4
  54.6 2.3 copy-start.10
  57.0 2.4 copy-start.8
  57.0 2.7 copy-start.5
  59.7 1.2 copy-start.7
  60.9 1.7 copy-start.6
  60.9 1.9 copy-start.9
  64.1 16.6 %copy-start.11 = (bf16[256,2048]{1,0:T(8,128)(2,1)S(1)}, bf16[256,2048]{1,0:T(8,128)(2,1)}, u32[]{:S(2)}) copy-start(bf16[256,2048]{1,0:T(8,128)(2,1)} %param.23) | copy-start | bytes 3145732
  84.9 0.7 copy-start.13
  84.9 34.8 %copy-start.3 = (bf16[128,2048]{1,0:T(8,128)(2,1)S(1)}, bf16[128,2048]{1,0:T(8,128)(2,1)}, u32[]{:S(2)}) copy-start(bf16[128,2048]{1,0:T(8,128)(2,1)} %param.16) | copy-start | bytes 1572868
  84.9 38.2 %copy-start.12 = (s32[128,4]{0,1:T(4,128)S(1)}, s32[128,4]{0,1:T(4,128)}, u32[]{:S(2)}) copy-start(s32[128,4]{0,1:T(4,128)} %param.25) | copy-start | bytes 6148
  85.0 106.5 %all-gather.5.cloned.1.call-start = ((), (), s32[]{:S(2)}) async-start(), calls=%async_computation.6 | async-start | bytes 4718592 | tf_op jit(solution)/shard_map/all_gather | solution.py:166
  123.1 148.4 %reduce-scatter.5.cloned.1.call-start = ((), (), s32[]{:S(2)}) async-start(), calls=%async_computation.7 | async-start | bytes 4718592 | tf_op jit(solution)/shard_map/reduce_scatter | solution.py:172
  190.5 15.9 %collective-permute-start = (bf16[640,2048]{1,0:T(8,128)(2,1)}, bf16[640,2048]{1,0:T(8,128)(2,1)}, u32[]{:S(2)}, u32[]{:S(2)}) collective-permute-start(bf16[640,2048]{1,0:T(8,128)(2,1)} %bitcast.130), channel_id=1, source_target_pairs={{0,1},{1,0},{2,3},{3,2},{4,5},{5,4},{6,7},{7,6},{8,9},{9,8},{10,11... | collective-permute-start | bytes 7864328 | tf_op jit(solution)/shard_map/ppermute | solution.py:198
  191.5 9.6 %copy-start.16 = (bf16[704,2048]{1,0:T(8,128)(2,1)S(1)}, bf16[704,2048]{1,0:T(8,128)(2,1)}, u32[]{:S(2)}) copy-start(bf16[704,2048]{1,0:T(8,128)(2,1)} %param.30) | copy-start | bytes 8650756
  206.4 7.6 %copy-start.17 = (bf16[1,704,2048]{2,1,0:T(8,128)(2,1)S(1)}, bf16[1,704,2048]{2,1,0:T(8,128)(2,1)}, u32[]{:S(2)}) copy-start(bf16[1,704,2048]{2,1,0:T(8,128)(2,1)} %param.28) | copy-start | bytes 8650756
  216.3 7.0 %collective-permute-start.1 = (bf16[640,2048]{1,0:T(8,128)(2,1)S(1)}, bf16[640,2048]{1,0:T(8,128)(2,1)S(1)}, u32[]{:S(2)}, u32[]{:S(2)}) collective-permute-start(bf16[640,2048]{1,0:T(8,128)(2,1)S(1)} %convolution_convert_fusion.2), channel_id=1, source_target_pairs={{0,1},{1,0},{2,3},{3,2},{4,5},{5,4},{6,7},{7,6},{8,9},{9,8},{10,11... | collective-permute-start | bytes 7864328 | tf_op jit(solution)/shard_map/ppermute | solution.py:209
  228.1 5.7 %copy-start.14 = (bf16[2048]{0:T(1024)(128)(2,1)S(1)}, bf16[2048]{0:T(1024)(128)(2,1)}, u32[]{:S(2)}) copy-start(bf16[2048]{0:T(1024)(128)(2,1)} %param.31) | copy-start | bytes 12292
  228.1 5.7 %copy-start.15 = (f32[128,4]{0,1:T(4,128)S(1)}, f32[128,4]{0,1:T(4,128)}, u32[]{:S(2)}) copy-start(f32[128,4]{0,1:T(4,128)} %param.26) | copy-start | bytes 6148
  228.1 43.4 %all-to-all-start.1 = ((bf16[64,10,16,128]{3,2,1,0:T(8,128)(2,1)}), bf16[64,10,16,128]{3,2,1,0:T(8,128)(2,1)}, u32[]{:S(2)}, u32[]{:S(2)}) async-start(bf16[64,10,16,128]{3,2,1,0:T(8,128)(2,1)} %bitcast.35), calls=%async_computation.3 | async-start | bytes 5242880 | tf_op jit(solution)/shard_map/all_to_all | solution.py:213
  233.8 42.1 %copy-start.1 = (bf16[3,2048,256]{2,1,0:T(8,128)(2,1)S(1)}, bf16[3,2048,256]{2,1,0:T(8,128)(2,1)}, u32[]{:S(2)}) copy-start(bf16[3,2048,256]{2,1,0:T(8,128)(2,1)} %param.21) | copy-start | bytes 9437188
Sparse Core Ops, SparseCore 0:
  10.9 35.6 all-gather.2
  85.1 34.5 reduce-scatter.2
  123.2 60.5 all-gather.4
  206.5 30.3 reduce-scatter.4

commit v5 on v4

--- a/solution.py
+++ b/solution.py
@@ -36,7 +36,7 @@
     head_count = queries.shape[1]
     head_size = queries.shape[2]
     key_count = keys_all.shape[0]
-    block_rows = math.gcd(row_count, 256)
+    block_rows = math.gcd(row_count, 512)
     scale = 1.0 / math.sqrt(head_size)
 
     def kernel(context_ref, query_ref, key_ref, value_ref, out_ref):

time: 283 us -> 288 us (1.018)
  Pallas kernels: 16.6 us -> 21 us
    pallas_call x1, Pallas kernels: 16.6 us -> 21 us  [attend(): pl.pallas_call(kernel, out_shape=jax.ShapeDtypeStruct((row_count, width),...]
where the time goes in v5:
time: 288 us; the launch traced here: 287 us
  waiting for transfers between devices  95.9 us (33%)
  blocking collectives  60.1 us (21%)
  matrix products  51 us (18%)
  other arithmetic  22.4 us (8%)
  Pallas kernels  21 us (7%)
  local copies, waits for them, and re-layouts  15.8 us (5%)
  between operations  14.1 us (5%)
  starting transfers between devices  7.12 us (2%)
    all_to_all x1, blocking collectives, per_device(): lax.all_to_all(buffer.reshape(tiles), ('tok', 'x'), 0, 0, tiled=True)  60.1 us
    all_to_all x1, waiting for transfers between devices, per_device(): lax.all_to_all(merged_own.reshape(tiles), ('tok', 'x'), 0, 0, tiled=True)  36.5 us
    reduce_scatter x1, waiting for transfers between devices, per_device(): lax.psum_scatter(jnp.dot(heads_out, out_weight, preferred_element_type=jn...  34.1 us
    all_gather x1, waiting for transfers between devices, per_device(): lax.all_gather(rms_scale(hidden_in, attn_gain), HEAD, axis=0, tiled=True)  25.2 us
    pallas_call x1, Pallas kernels, attend(): pl.pallas_call(kernel, out_shape=jax.ShapeDtypeStruct((row_count, width),...  21 us
    dot_general x2, matrix products, half_expert(): inner = jnp.dot(rows, w_experts_in[0], preferred_element_type=jnp.float32)  14.3 us
    dot_general x1, matrix products, per_device(): jnp.einsum('td,dcf->tcf', lax.all_gather(mixed, HEAD, axis=0, tiled=True)...  9.58 us
    unnamed x43, local copies, waits for them, and re-layouts  7.47 us
  transfers between devices with their start and end apart: 7, of which 3 were waited for; matrix products, arithmetic and copies ran while one was open for 19% of the time, Pallas kernels for 0%

profile of v5, /device:TPU:1, one launch (start us, length us, event | category | flops | bytes accessed | tf_op | source)
XLA Modules:
  0.0 287.4 jit_solution(16386158972761547554)
XLA Ops:
  7.4 1.3 fusion.35
  8.7 2.0 fusion.37
  12.8 3.6 %gather_fusion = bf16[16,2,128,256]{3,2,1,0:T(8,128)(2,1)} fusion(bf16[2,16,128,256]{3,2,1,0:T(8,128)(2,1)} %param.19, s32[1024]{0:T(1024)S(1)} %pad_clamp_fusion), kind=kCustom, calls=%fused_computation | custom fusion | bytes 4194368 | tf_op jit(solution)/shard_map/jit(_take)/gather | solution.py:148
  16.7 2.9 %fusion.50 = (f32[1024,128]{1,0:T(8,128)}, f32[1024,128]{1,0:T(8,128)}) fusion(f32[1024,64]{1,0:T(8,128)S(1)} %broadcast_multiply_fusion), kind=kLoop, calls=%fused_computation.76 | loop fusion | flops 131072 | bytes 1310720 | tf_op jit(solution)/shard_map/cos | solution.py:31
  19.9 1.5 fusion.61
  21.3 25.2 %all-gather.3.cloned.1.call-done = bf16[1024,2048]{1,0:T(8,128)(2,1)} async-done(((bf16[128,2048]{1,0:T(8,128)(2,1)}), bf16[1024,2048]{1,0:T(8,128)(2,1)}) %all-gather.3.cloned.1.call-update) | async-done | bytes 4194320 | tf_op jit(solution)/shard_map/all_gather | solution.py:132
  46.6 5.2 %add_bitcast_fusion = f32[3,1024,256]{2,1,0:T(8,128)S(1)} fusion(bf16[3,2048,256]{2,1,0:T(8,128)(2,1)S(1)} %copy-done, bf16[1024,2048]{1,0:T(8,128)(2,1)} %all-gather.3.cloned.1.call-done, f32[3,256]{1,0:T(4,128)S(1)} %convert_element_type.106), kind=kOutput, calls=%fused_computation.15 | convolution fusion | flops 3222011904 | bytes 10488832 | tf_op jit(solution)/shard_map/td,cdf->ctf/dot_general | solution.py:136
  54.6 2.3 slice_negate_fusion
  57.0 2.3 maximum_multiply_fusion.1
  59.7 1.2 fusion.42
  60.9 1.3 pad_maximum_fusion.key_ref
  62.9 1.3 pad_maximum_fusion.1.value_ref
  64.1 21.0 %shard_map.154 = bf16[1024,256]{1,0:T(8,128)(2,1)} custom-call(s32[1]{0:T(128)} %copy.71.context_ref, bf16[1024,256]{1,0:T(8,128)(2,1)} %get-tuple-element.6.query_ref, bf16[3072,256]{1,0:T(8,128)(2,1)} %pad_maximum_fusion.key_ref, bf16[3072,256]{1,0:T(8,128)(2,1)} %pad_maximum_fusion.1.value_ref), custom_call_target="tpu_custom_call" | custom-call | tf_op jit(solution)/shard_map/pallas_call | solution.py:85
  85.1 4.3 %convolution_convert_fusion.1 = bf16[1024,2048]{1,0:T(8,128)(2,1)} fusion(bf16[1024,256]{1,0:T(8,128)(2,1)} %shard_map.154, bf16[256,2048]{1,0:T(8,128)(2,1)S(1)} %copy-done.11), kind=kOutput, calls=%fused_computation.11 | convolution fusion | flops 1075838976 | bytes 5767168 | tf_op jit(solution)/shard_map/dot_general | solution.py:157
  90.0 34.1 %reduce-scatter.3.cloned.1.call-done = bf16[128,2048]{1,0:T(8,128)(2,1)} async-done(((bf16[1024,2048]{1,0:T(8,128)(2,1)}), bf16[128,2048]{1,0:T(8,128)(2,1)}) %reduce-scatter.3.cloned.1.call-update) | async-done | bytes 524304 | tf_op jit(solution)/shard_map/reduce_scatter | solution.py:156
  124.1 1.3 fusion.39
  125.4 2.0 fusion.41
  127.9 1.2 reduce-window.6
  129.8 1.9 fusion.26
  132.5 60.1 %all_to_all.10 = bf16[64,10,16,128]{3,2,1,0:T(8,128)(2,1)S(1)} all-to-all(bf16[64,10,16,128]{3,2,1,0:T(8,128)(2,1)S(1)} %bitcast.134), channel_id=1, replica_groups=mesh['tok'=16,'x'=4,'core'=2] {'tok','x'}, dimensions={0} | all-to-all | bytes 5242880 | tf_op jit(solution)/shard_map/all_to_all | solution.py:195
  192.6 2.2 copy.70
  195.9 9.6 %fusion.4 = f32[1024,2,704]{0,2,1:T(8,128)S(1)} fusion(bf16[2048,2,704]{0,2,1:T(8,128)(2,1)} %param.29, bf16[1024,2048]{1,0:T(8,128)(2,1)} %all-gather.5.cloned.1.call-done), kind=kOutput, calls=%fused_computation.6 | convolution fusion | flops 5905580032 | bytes 15728640 | tf_op jit(solution)/shard_map/td,dcf->tcf/dot_general | solution.py:164
  205.5 5.3 %convolution_convert_fusion = bf16[1024,2048]{1,0:T(8,128)(2,1)} fusion(bf16[704,2048]{1,0:T(8,128)(2,1)S(1)} %copy-done.16, f32[1024,2,704]{0,2,1:T(8,128)S(1)} %fusion.4), kind=kOutput, calls=%fused_computation.10 | convolution fusion | flops 2959212544 | bytes 12845056 | tf_op jit(solution)/shard_map/dot_general | solution.py:171
  210.8 7.5 %fusion = f32[640,1408]{1,0:T(8,128)S(1)} fusion(bf16[640,2048]{1,0:T(8,128)(2,1)} %collective-permute-done, bf16[1,2048,1408]{2,1,0:T(8,128)(2,1)} %param.27), kind=kOutput, calls=%fused_computation.1 | convolution fusion | flops 3690987520 | bytes 11993088 | tf_op jit(solution)/shard_map/dot_general | solution.py:201
  218.4 2.3 convolution_convert_fusion.2
  221.0 6.7 %fusion.2 = f32[640,1408]{1,0:T(8,128)S(1)} fusion(bf16[1,2048,1408]{2,1,0:T(8,128)(2,1)} %param.27, bf16[80,8,16,128]{3,2,1,0:T(8,128)(2,1)S(1)} %bitcast.133), kind=kOutput, calls=%fused_computation.3 | convolution fusion | flops 3690987520 | bytes 11993088 | tf_op jit(solution)/shard_map/dot_general | solution.py:201
  227.7 2.4 fusion.12
  230.1 2.4 copy.53
  232.5 5.7 %all-to-all-start.1 = ((bf16[64,10,16,128]{3,2,1,0:T(8,128)(2,1)}), bf16[64,10,16,128]{3,2,1,0:T(8,128)(2,1)}, u32[]{:S(2)}, u32[]{:S(2)}) async-start(bf16[64,10,16,128]{3,2,1,0:T(8,128)(2,1)} %bitcast.35), calls=%async_computation.3 | async-start | bytes 5242880 | tf_op jit(solution)/shard_map/all_to_all | solution.py:213
  238.5 1.4 fusion.34
  239.9 36.5 %all-to-all-done.1 = bf16[64,10,16,128]{3,2,1,0:T(8,128)(2,1)} async-done(((bf16[64,10,16,128]{3,2,1,0:T(8,128)(2,1)}), bf16[64,10,16,128]{3,2,1,0:T(8,128)(2,1)}, u32[]{:S(2)}, u32[]{:S(2)}) %all-to-all-start.1) | async-done | bytes 2621472 | tf_op jit(solution)/shard_map/all_to_all | solution.py:213
  276.4 4.5 %fusion.21 = bf16[128,2048]{1,0:T(8,128)(2,1)} fusion(f32[128,640]{1,0:T(8,128)S(1)} %select_reduce_fusion, bf16[80,8,16,128]{3,2,1,0:T(8,128)(2,1)} %bitcast.37, bf16[128,2048]{1,0:T(8,128)(2,1)} %reduce-scatter.5.cloned.1.call-done, f32[128]{0:T(128)S(1)} %fusion.34, bf16[128,2048]{1,0:T(8,128)(2,1)} %reduce-scatter.3.cloned.1.call-done, ...), kind=kOutput, calls=%fused_computation.28 | convolution fusion | flops 2015887360 | bytes 5046784 | tf_op jit(solution)/shard_map/dot_general | solution.py:225
  (84 shorter events, 10.9 us)
Async XLA Ops:
  6.5 40.0 %copy-start = (bf16[3,2048,256]{2,1,0:T(8,128)(2,1)S(1)}, bf16[3,2048,256]{2,1,0:T(8,128)(2,1)}, u32[]{:S(2)}) copy-start(bf16[3,2048,256]{2,1,0:T(8,128)(2,1)} %param.21) | copy-start | bytes 9437188
  6.5 40.0 %all-gather.3.cloned.1.call-start = ((), (), s32[]{:S(2)}) async-start(), calls=%async_computation.4 | async-start | bytes 4718592 | tf_op jit(solution)/shard_map/all_gather | solution.py:132
  10.8 113.3 %reduce-scatter.3.cloned.1.call-start = ((), (), s32[]{:S(2)}) async-start(), calls=%async_computation.5 | async-start | bytes 4718592 | tf_op jit(solution)/shard_map/reduce_scatter | solution.py:156
  12.8 6.7 %copy-start.18 = (s32[1,16]{1,0:T(1,128)S(1)}, s32[1,16]{1,0:T(1,128)}, u32[]{:S(2)}) copy-start(s32[1,16]{1,0:T(1,128)} %param.18) | copy-start | bytes 196
  16.5 3.1 %copy-start.2 = (bf16[16,2,128,256]{3,2,1,0:T(8,128)(2,1)S(1)}, bf16[16,2,128,256]{3,2,1,0:T(8,128)(2,1)}, u32[]{:S(2)}) copy-start(bf16[16,2,128,256]{3,2,1,0:T(8,128)(2,1)} %gather_fusion) | copy-start | bytes 6291460
  51.8 1.8 copy-start.4
  54.6 2.3 copy-start.10
  57.0 2.4 copy-start.8
  57.0 2.7 copy-start.5
  59.7 1.2 copy-start.7
  60.9 1.7 copy-start.6
  60.9 1.9 copy-start.9
  64.1 21.0 %copy-start.11 = (bf16[256,2048]{1,0:T(8,128)(2,1)S(1)}, bf16[256,2048]{1,0:T(8,128)(2,1)}, u32[]{:S(2)}) copy-start(bf16[256,2048]{1,0:T(8,128)(2,1)} %param.23) | copy-start | bytes 3145732
  89.3 0.7 copy-start.13
  89.3 34.8 %copy-start.3 = (bf16[128,2048]{1,0:T(8,128)(2,1)S(1)}, bf16[128,2048]{1,0:T(8,128)(2,1)}, u32[]{:S(2)}) copy-start(bf16[128,2048]{1,0:T(8,128)(2,1)} %param.16) | copy-start | bytes 1572868
  89.3 38.2 %copy-start.12 = (s32[128,4]{0,1:T(4,128)S(1)}, s32[128,4]{0,1:T(4,128)}, u32[]{:S(2)}) copy-start(s32[128,4]{0,1:T(4,128)} %param.25) | copy-start | bytes 6148
  89.4 106.5 %all-gather.5.cloned.1.call-start = ((), (), s32[]{:S(2)}) async-start(), calls=%async_computation.6 | async-start | bytes 4718592 | tf_op jit(solution)/shard_map/all_gather | solution.py:166
  127.5 148.9 %reduce-scatter.5.cloned.1.call-start = ((), (), s32[]{:S(2)}) async-start(), calls=%async_computation.7 | async-start | bytes 4718592 | tf_op jit(solution)/shard_map/reduce_scatter | solution.py:172
  194.9 15.9 %collective-permute-start = (bf16[640,2048]{1,0:T(8,128)(2,1)}, bf16[640,2048]{1,0:T(8,128)(2,1)}, u32[]{:S(2)}, u32[]{:S(2)}) collective-permute-start(bf16[640,2048]{1,0:T(8,128)(2,1)} %bitcast.130), channel_id=1, source_target_pairs={{0,1},{1,0},{2,3},{3,2},{4,5},{5,4},{6,7},{7,6},{8,9},{9,8},{10,11... | collective-permute-start | bytes 7864328 | tf_op jit(solution)/shard_map/ppermute | solution.py:198
  195.9 9.6 %copy-start.16 = (bf16[704,2048]{1,0:T(8,128)(2,1)S(1)}, bf16[704,2048]{1,0:T(8,128)(2,1)}, u32[]{:S(2)}) copy-start(bf16[704,2048]{1,0:T(8,128)(2,1)} %param.30) | copy-start | bytes 8650756
  210.8 7.6 %copy-start.17 = (bf16[1,704,2048]{2,1,0:T(8,128)(2,1)S(1)}, bf16[1,704,2048]{2,1,0:T(8,128)(2,1)}, u32[]{:S(2)}) copy-start(bf16[1,704,2048]{2,1,0:T(8,128)(2,1)} %param.28) | copy-start | bytes 8650756
  220.6 7.1 %collective-permute-start.1 = (bf16[640,2048]{1,0:T(8,128)(2,1)S(1)}, bf16[640,2048]{1,0:T(8,128)(2,1)S(1)}, u32[]{:S(2)}, u32[]{:S(2)}) collective-permute-start(bf16[640,2048]{1,0:T(8,128)(2,1)S(1)} %convolution_convert_fusion.2), channel_id=1, source_target_pairs={{0,1},{1,0},{2,3},{3,2},{4,5},{5,4},{6,7},{7,6},{8,9},{9,8},{10,11... | collective-permute-start | bytes 7864328 | tf_op jit(solution)/shard_map/ppermute | solution.py:209
  232.5 5.7 %copy-start.14 = (bf16[2048]{0:T(1024)(128)(2,1)S(1)}, bf16[2048]{0:T(1024)(128)(2,1)}, u32[]{:S(2)}) copy-start(bf16[2048]{0:T(1024)(128)(2,1)} %param.31) | copy-start | bytes 12292
  232.5 5.7 %copy-start.15 = (f32[128,4]{0,1:T(4,128)S(1)}, f32[128,4]{0,1:T(4,128)}, u32[]{:S(2)}) copy-start(f32[128,4]{0,1:T(4,128)} %param.26) | copy-start | bytes 6148
  232.5 43.9 %all-to-all-start.1 = ((bf16[64,10,16,128]{3,2,1,0:T(8,128)(2,1)}), bf16[64,10,16,128]{3,2,1,0:T(8,128)(2,1)}, u32[]{:S(2)}, u32[]{:S(2)}) async-start(bf16[64,10,16,128]{3,2,1,0:T(8,128)(2,1)} %bitcast.35), calls=%async_computation.3 | async-start | bytes 5242880 | tf_op jit(solution)/shard_map/all_to_all | solution.py:213
  238.2 42.6 %copy-start.1 = (bf16[3,2048,256]{2,1,0:T(8,128)(2,1)S(1)}, bf16[3,2048,256]{2,1,0:T(8,128)(2,1)}, u32[]{:S(2)}) copy-start(bf16[3,2048,256]{2,1,0:T(8,128)(2,1)} %param.21) | copy-start | bytes 9437188
Sparse Core Ops, SparseCore 0:
  10.9 35.6 all-gather.2
  89.5 34.5 reduce-scatter.2
  127.6 60.5 all-gather.4
  210.9 30.5 reduce-scatter.4

commit v6 on v5

--- a/solution.py
+++ b/solution.py
@@ -36,7 +36,7 @@
     head_count = queries.shape[1]
     head_size = queries.shape[2]
     key_count = keys_all.shape[0]
-    block_rows = math.gcd(row_count, 512)
+    block_rows = math.gcd(row_count, 128)
     scale = 1.0 / math.sqrt(head_size)
 
     def kernel(context_ref, query_ref, key_ref, value_ref, out_ref):

time: 288 us -> 287 us (level)
  no operation moved by 1% of the time
where the time goes in v6:
time: 287 us; the launch traced here: 286 us
  waiting for transfers between devices  95.4 us (33%)
  blocking collectives  60 us (21%)
  matrix products  51 us (18%)
  other arithmetic  22.4 us (8%)
  Pallas kernels  20.2 us (7%)
  local copies, waits for them, and re-layouts  15.6 us (5%)
  between operations  14.1 us (5%)
  starting transfers between devices  7.29 us (3%)
    all_to_all x1, blocking collectives, per_device(): lax.all_to_all(buffer.reshape(tiles), ('tok', 'x'), 0, 0, tiled=True)  60 us
    all_to_all x1, waiting for transfers between devices, per_device(): lax.all_to_all(merged_own.reshape(tiles), ('tok', 'x'), 0, 0, tiled=True)  36 us
    reduce_scatter x1, waiting for transfers between devices, per_device(): lax.psum_scatter(jnp.dot(heads_out, out_weight, preferred_element_type=jn...  34.1 us
    all_gather x1, waiting for transfers between devices, per_device(): lax.all_gather(rms_scale(hidden_in, attn_gain), HEAD, axis=0, tiled=True)  25.2 us
    pallas_call x1, Pallas kernels, attend(): pl.pallas_call(kernel, out_shape=jax.ShapeDtypeStruct((row_count, width),...  20.2 us
    dot_general x2, matrix products, half_expert(): inner = jnp.dot(rows, w_experts_in[0], preferred_element_type=jnp.float32)  14.2 us
    dot_general x1, matrix products, per_device(): jnp.einsum('td,dcf->tcf', lax.all_gather(mixed, HEAD, axis=0, tiled=True)...  9.59 us
    unnamed x43, local copies, waits for them, and re-layouts  7.29 us
  transfers between devices with their start and end apart: 7, of which 3 were waited for; matrix products, arithmetic and copies ran while one was open for 19% of the time, Pallas kernels for 0%

profile of v6, /device:TPU:1, one launch (start us, length us, event | category | flops | bytes accessed | tf_op | source)
XLA Modules:
  0.0 286.0 jit_solution(3361815553432019772)
XLA Ops:
  7.4 1.3 fusion.35
  8.7 2.0 fusion.37
  12.8 3.6 %gather_fusion = bf16[16,2,128,256]{3,2,1,0:T(8,128)(2,1)} fusion(bf16[2,16,128,256]{3,2,1,0:T(8,128)(2,1)} %param.19, s32[1024]{0:T(1024)S(1)} %pad_clamp_fusion), kind=kCustom, calls=%fused_computation | custom fusion | bytes 4194368 | tf_op jit(solution)/shard_map/jit(_take)/gather | solution.py:148
  16.7 2.9 %fusion.50 = (f32[1024,128]{1,0:T(8,128)}, f32[1024,128]{1,0:T(8,128)}) fusion(f32[1024,64]{1,0:T(8,128)S(1)} %broadcast_multiply_fusion), kind=kLoop, calls=%fused_computation.76 | loop fusion | flops 131072 | bytes 1310720 | tf_op jit(solution)/shard_map/cos | solution.py:31
  19.9 1.5 fusion.61
  21.3 25.2 %all-gather.3.cloned.1.call-done = bf16[1024,2048]{1,0:T(8,128)(2,1)} async-done(((bf16[128,2048]{1,0:T(8,128)(2,1)}), bf16[1024,2048]{1,0:T(8,128)(2,1)}) %all-gather.3.cloned.1.call-update) | async-done | bytes 4194320 | tf_op jit(solution)/shard_map/all_gather | solution.py:132
  46.6 5.2 %add_bitcast_fusion = f32[3,1024,256]{2,1,0:T(8,128)S(1)} fusion(bf16[3,2048,256]{2,1,0:T(8,128)(2,1)S(1)} %copy-done, bf16[1024,2048]{1,0:T(8,128)(2,1)} %all-gather.3.cloned.1.call-done, f32[3,256]{1,0:T(4,128)S(1)} %convert_element_type.106), kind=kOutput, calls=%fused_computation.15 | convolution fusion | flops 3222011904 | bytes 10488832 | tf_op jit(solution)/shard_map/td,cdf->ctf/dot_general | solution.py:136
  54.6 2.3 slice_negate_fusion
  57.0 2.3 maximum_multiply_fusion.1
  59.7 1.2 fusion.42
  60.9 1.3 pad_maximum_fusion.key_ref
  62.9 1.3 pad_maximum_fusion.1.value_ref
  64.1 20.2 %shard_map.154 = bf16[1024,256]{1,0:T(8,128)(2,1)} custom-call(s32[1]{0:T(128)} %copy.71.context_ref, bf16[1024,256]{1,0:T(8,128)(2,1)} %get-tuple-element.6.query_ref, bf16[3072,256]{1,0:T(8,128)(2,1)} %pad_maximum_fusion.key_ref, bf16[3072,256]{1,0:T(8,128)(2,1)} %pad_maximum_fusion.1.value_ref), custom_call_target="tpu_custom_call" | custom-call | tf_op jit(solution)/shard_map/pallas_call | solution.py:85
  84.3 4.3 %convolution_convert_fusion.1 = bf16[1024,2048]{1,0:T(8,128)(2,1)} fusion(bf16[1024,256]{1,0:T(8,128)(2,1)} %shard_map.154, bf16[256,2048]{1,0:T(8,128)(2,1)S(1)} %copy-done.11), kind=kOutput, calls=%fused_computation.11 | convolution fusion | flops 1075838976 | bytes 5767168 | tf_op jit(solution)/shard_map/dot_general | solution.py:157
  89.2 34.1 %reduce-scatter.3.cloned.1.call-done = bf16[128,2048]{1,0:T(8,128)(2,1)} async-done(((bf16[1024,2048]{1,0:T(8,128)(2,1)}), bf16[128,2048]{1,0:T(8,128)(2,1)}) %reduce-scatter.3.cloned.1.call-update) | async-done | bytes 524304 | tf_op jit(solution)/shard_map/reduce_scatter | solution.py:156
  123.3 1.3 fusion.39
  124.6 2.0 fusion.41
  127.1 1.2 reduce-window.6
  129.1 1.9 fusion.26
  131.8 60.0 %all_to_all.10 = bf16[64,10,16,128]{3,2,1,0:T(8,128)(2,1)S(1)} all-to-all(bf16[64,10,16,128]{3,2,1,0:T(8,128)(2,1)S(1)} %bitcast.134), channel_id=1, replica_groups=mesh['tok'=16,'x'=4,'core'=2] {'tok','x'}, dimensions={0} | all-to-all | bytes 5242880 | tf_op jit(solution)/shard_map/all_to_all | solution.py:195
  191.8 2.2 copy.70
  195.0 9.6 %fusion.4 = f32[1024,2,704]{0,2,1:T(8,128)S(1)} fusion(bf16[2048,2,704]{0,2,1:T(8,128)(2,1)} %param.29, bf16[1024,2048]{1,0:T(8,128)(2,1)} %all-gather.5.cloned.1.call-done), kind=kOutput, calls=%fused_computation.6 | convolution fusion | flops 5905580032 | bytes 15728640 | tf_op jit(solution)/shard_map/td,dcf->tcf/dot_general | solution.py:164
  204.6 5.3 %convolution_convert_fusion = bf16[1024,2048]{1,0:T(8,128)(2,1)} fusion(bf16[704,2048]{1,0:T(8,128)(2,1)S(1)} %copy-done.16, f32[1024,2,704]{0,2,1:T(8,128)S(1)} %fusion.4), kind=kOutput, calls=%fused_computation.10 | convolution fusion | flops 2959212544 | bytes 12845056 | tf_op jit(solution)/shard_map/dot_general | solution.py:171
  209.9 7.5 %fusion = f32[640,1408]{1,0:T(8,128)S(1)} fusion(bf16[640,2048]{1,0:T(8,128)(2,1)} %collective-permute-done, bf16[1,2048,1408]{2,1,0:T(8,128)(2,1)} %param.27), kind=kOutput, calls=%fused_computation.1 | convolution fusion | flops 3690987520 | bytes 11993088 | tf_op jit(solution)/shard_map/dot_general | solution.py:201
  217.5 2.3 convolution_convert_fusion.2
  220.1 6.7 %fusion.2 = f32[640,1408]{1,0:T(8,128)S(1)} fusion(bf16[1,2048,1408]{2,1,0:T(8,128)(2,1)} %param.27, bf16[80,8,16,128]{3,2,1,0:T(8,128)(2,1)S(1)} %bitcast.133), kind=kOutput, calls=%fused_computation.3 | convolution fusion | flops 3690987520 | bytes 11993088 | tf_op jit(solution)/shard_map/dot_general | solution.py:201
  226.8 2.4 fusion.12
  229.2 2.4 copy.53
  231.6 5.7 %all-to-all-start.1 = ((bf16[64,10,16,128]{3,2,1,0:T(8,128)(2,1)}), bf16[64,10,16,128]{3,2,1,0:T(8,128)(2,1)}, u32[]{:S(2)}, u32[]{:S(2)}) async-start(bf16[64,10,16,128]{3,2,1,0:T(8,128)(2,1)} %bitcast.35), calls=%async_computation.3 | async-start | bytes 5242880 | tf_op jit(solution)/shard_map/all_to_all | solution.py:213
  237.6 1.4 fusion.34
  239.0 36.0 %all-to-all-done.1 = bf16[64,10,16,128]{3,2,1,0:T(8,128)(2,1)} async-done(((bf16[64,10,16,128]{3,2,1,0:T(8,128)(2,1)}), bf16[64,10,16,128]{3,2,1,0:T(8,128)(2,1)}, u32[]{:S(2)}, u32[]{:S(2)}) %all-to-all-start.1) | async-done | bytes 2621472 | tf_op jit(solution)/shard_map/all_to_all | solution.py:213
  275.0 4.5 %fusion.21 = bf16[128,2048]{1,0:T(8,128)(2,1)} fusion(f32[128,640]{1,0:T(8,128)S(1)} %select_reduce_fusion, bf16[80,8,16,128]{3,2,1,0:T(8,128)(2,1)} %bitcast.37, bf16[128,2048]{1,0:T(8,128)(2,1)} %reduce-scatter.5.cloned.1.call-done, f32[128]{0:T(128)S(1)} %fusion.34, bf16[128,2048]{1,0:T(8,128)(2,1)} %reduce-scatter.3.cloned.1.call-done, ...), kind=kOutput, calls=%fused_computation.28 | convolution fusion | flops 2015887360 | bytes 5046784 | tf_op jit(solution)/shard_map/dot_general | solution.py:225
  (84 shorter events, 10.9 us)
Async XLA Ops:
  6.5 40.0 %copy-start = (bf16[3,2048,256]{2,1,0:T(8,128)(2,1)S(1)}, bf16[3,2048,256]{2,1,0:T(8,128)(2,1)}, u32[]{:S(2)}) copy-start(bf16[3,2048,256]{2,1,0:T(8,128)(2,1)} %param.21) | copy-start | bytes 9437188
  6.5 40.0 %all-gather.3.cloned.1.call-start = ((), (), s32[]{:S(2)}) async-start(), calls=%async_computation.4 | async-start | bytes 4718592 | tf_op jit(solution)/shard_map/all_gather | solution.py:132
  10.8 112.5 %reduce-scatter.3.cloned.1.call-start = ((), (), s32[]{:S(2)}) async-start(), calls=%async_computation.5 | async-start | bytes 4718592 | tf_op jit(solution)/shard_map/reduce_scatter | solution.py:156
  12.8 6.7 %copy-start.18 = (s32[1,16]{1,0:T(1,128)S(1)}, s32[1,16]{1,0:T(1,128)}, u32[]{:S(2)}) copy-start(s32[1,16]{1,0:T(1,128)} %param.18) | copy-start | bytes 196
  16.5 3.1 %copy-start.2 = (bf16[16,2,128,256]{3,2,1,0:T(8,128)(2,1)S(1)}, bf16[16,2,128,256]{3,2,1,0:T(8,128)(2,1)}, u32[]{:S(2)}) copy-start(bf16[16,2,128,256]{3,2,1,0:T(8,128)(2,1)} %gather_fusion) | copy-start | bytes 6291460
  51.8 1.8 copy-start.4
  54.6 2.3 copy-start.10
  57.0 2.4 copy-start.8
  57.0 2.7 copy-start.5
  59.7 1.2 copy-start.7
  60.9 1.7 copy-start.6
  60.9 1.9 copy-start.9
  64.1 20.2 %copy-start.11 = (bf16[256,2048]{1,0:T(8,128)(2,1)S(1)}, bf16[256,2048]{1,0:T(8,128)(2,1)}, u32[]{:S(2)}) copy-start(bf16[256,2048]{1,0:T(8,128)(2,1)} %param.23) | copy-start | bytes 3145732
  88.5 0.7 copy-start.13
  88.5 34.8 %copy-start.3 = (bf16[128,2048]{1,0:T(8,128)(2,1)S(1)}, bf16[128,2048]{1,0:T(8,128)(2,1)}, u32[]{:S(2)}) copy-start(bf16[128,2048]{1,0:T(8,128)(2,1)} %param.16) | copy-start | bytes 1572868
  88.5 38.2 %copy-start.12 = (s32[128,4]{0,1:T(4,128)S(1)}, s32[128,4]{0,1:T(4,128)}, u32[]{:S(2)}) copy-start(s32[128,4]{0,1:T(4,128)} %param.25) | copy-start | bytes 6148
  88.6 106.4 %all-gather.5.cloned.1.call-start = ((), (), s32[]{:S(2)}) async-start(), calls=%async_computation.6 | async-start | bytes 4718592 | tf_op jit(solution)/shard_map/all_gather | solution.py:166
  126.7 148.3 %reduce-scatter.5.cloned.1.call-start = ((), (), s32[]{:S(2)}) async-start(), calls=%async_computation.7 | async-start | bytes 4718592 | tf_op jit(solution)/shard_map/reduce_scatter | solution.py:172
  194.0 15.9 %collective-permute-start = (bf16[640,2048]{1,0:T(8,128)(2,1)}, bf16[640,2048]{1,0:T(8,128)(2,1)}, u32[]{:S(2)}, u32[]{:S(2)}) collective-permute-start(bf16[640,2048]{1,0:T(8,128)(2,1)} %bitcast.130), channel_id=1, source_target_pairs={{0,1},{1,0},{2,3},{3,2},{4,5},{5,4},{6,7},{7,6},{8,9},{9,8},{10,11... | collective-permute-start | bytes 7864328 | tf_op jit(solution)/shard_map/ppermute | solution.py:198
  195.0 9.6 %copy-start.16 = (bf16[704,2048]{1,0:T(8,128)(2,1)S(1)}, bf16[704,2048]{1,0:T(8,128)(2,1)}, u32[]{:S(2)}) copy-start(bf16[704,2048]{1,0:T(8,128)(2,1)} %param.30) | copy-start | bytes 8650756
  209.9 7.6 %copy-start.17 = (bf16[1,704,2048]{2,1,0:T(8,128)(2,1)S(1)}, bf16[1,704,2048]{2,1,0:T(8,128)(2,1)}, u32[]{:S(2)}) copy-start(bf16[1,704,2048]{2,1,0:T(8,128)(2,1)} %param.28) | copy-start | bytes 8650756
  219.8 7.0 %collective-permute-start.1 = (bf16[640,2048]{1,0:T(8,128)(2,1)S(1)}, bf16[640,2048]{1,0:T(8,128)(2,1)S(1)}, u32[]{:S(2)}, u32[]{:S(2)}) collective-permute-start(bf16[640,2048]{1,0:T(8,128)(2,1)S(1)} %convolution_convert_fusion.2), channel_id=1, source_target_pairs={{0,1},{1,0},{2,3},{3,2},{4,5},{5,4},{6,7},{7,6},{8,9},{9,8},{10,11... | collective-permute-start | bytes 7864328 | tf_op jit(solution)/shard_map/ppermute | solution.py:209
  231.6 5.7 %copy-start.14 = (bf16[2048]{0:T(1024)(128)(2,1)S(1)}, bf16[2048]{0:T(1024)(128)(2,1)}, u32[]{:S(2)}) copy-start(bf16[2048]{0:T(1024)(128)(2,1)} %param.31) | copy-start | bytes 12292
  231.6 5.7 %copy-start.15 = (f32[128,4]{0,1:T(4,128)S(1)}, f32[128,4]{0,1:T(4,128)}, u32[]{:S(2)}) copy-start(f32[128,4]{0,1:T(4,128)} %param.26) | copy-start | bytes 6148
  231.6 43.4 %all-to-all-start.1 = ((bf16[64,10,16,128]{3,2,1,0:T(8,128)(2,1)}), bf16[64,10,16,128]{3,2,1,0:T(8,128)(2,1)}, u32[]{:S(2)}, u32[]{:S(2)}) async-start(bf16[64,10,16,128]{3,2,1,0:T(8,128)(2,1)} %bitcast.35), calls=%async_computation.3 | async-start | bytes 5242880 | tf_op jit(solution)/shard_map/all_to_all | solution.py:213
  237.3 42.1 %copy-start.1 = (bf16[3,2048,256]{2,1,0:T(8,128)(2,1)S(1)}, bf16[3,2048,256]{2,1,0:T(8,128)(2,1)}, u32[]{:S(2)}) copy-start(bf16[3,2048,256]{2,1,0:T(8,128)(2,1)} %param.21) | copy-start | bytes 9437188
Sparse Core Ops, SparseCore 0:
  10.9 35.6 all-gather.2
  88.7 34.5 reduce-scatter.2
  126.8 60.4 all-gather.4
  210.0 30.3 reduce-scatter.4

commit v7 on v4

--- a/solution.py
+++ b/solution.py
@@ -67,15 +67,16 @@
         )
         cached_weights = jnp.exp(cached_scores - largest)
         new_weights = jnp.exp(new_scores - largest)
-        total = jnp.sum(cached_weights, axis=-1, keepdims=True) + jnp.sum(
-            new_weights, axis=-1, keepdims=True
+        total = 1.0 / (
+            jnp.sum(cached_weights, axis=-1, keepdims=True)
+            + jnp.sum(new_weights, axis=-1, keepdims=True)
         )
         out = jnp.dot(
-            (cached_weights / total).astype(jnp.bfloat16),
+            (cached_weights * total).astype(jnp.bfloat16),
             value_ref[:span_len, :],
             preferred_element_type=jnp.float32,
         ) + jnp.dot(
-            (new_weights / total).astype(jnp.bfloat16),
+            (new_weights * total).astype(jnp.bfloat16),
             value_ref[span_len:, :],
             preferred_element_type=jnp.float32,
         )

time: 283 us -> 283 us (level)
  no operation moved by 1% of the time
where the time goes in v7:
time: 283 us; the launch traced here: 282 us
  waiting for transfers between devices  95.4 us (34%)
  blocking collectives  60.1 us (21%)
  matrix products  51 us (18%)
  other arithmetic  22.4 us (8%)
  Pallas kernels  16.6 us (6%)
  local copies, waits for them, and re-layouts  15.6 us (6%)
  between operations  14.1 us (5%)
  starting transfers between devices  7.29 us (3%)
    all_to_all x1, blocking collectives, per_device(): lax.all_to_all(buffer.reshape(tiles), ('tok', 'x'), 0, 0, tiled=True)  60.1 us
    all_to_all x1, waiting for transfers between devices, per_device(): lax.all_to_all(merged_own.reshape(tiles), ('tok', 'x'), 0, 0, tiled=True)  36 us
    reduce_scatter x1, waiting for transfers between devices, per_device(): lax.psum_scatter(jnp.dot(heads_out, out_weight, preferred_element_type=jn...  34.1 us
    all_gather x1, waiting for transfers between devices, per_device(): lax.all_gather(rms_scale(hidden_in, attn_gain), HEAD, axis=0, tiled=True)  25.2 us
    pallas_call x1, Pallas kernels, attend(): pl.pallas_call(kernel, out_shape=jax.ShapeDtypeStruct((row_count, width),...  16.6 us
    dot_general x2, matrix products, half_expert(): inner = jnp.dot(rows, w_experts_in[0], preferred_element_type=jnp.float32)  14.2 us
    dot_general x1, matrix products, per_device(): jnp.einsum('td,dcf->tcf', lax.all_gather(mixed, HEAD, axis=0, tiled=True)...  9.58 us
    unnamed x43, local copies, waits for them, and re-layouts  7.29 us
  transfers between devices with their start and end apart: 7, of which 3 were waited for; matrix products, arithmetic and copies ran while one was open for 19% of the time, Pallas kernels for 0%

profile of v7, /device:TPU:1, one launch (start us, length us, event | category | flops | bytes accessed | tf_op | source)
XLA Modules:
  0.0 282.5 jit_solution(12360558060024802479)
XLA Ops:
  7.4 1.3 fusion.35
  8.7 2.0 fusion.37
  12.8 3.6 %gather_fusion = bf16[16,2,128,256]{3,2,1,0:T(8,128)(2,1)} fusion(bf16[2,16,128,256]{3,2,1,0:T(8,128)(2,1)} %param.19, s32[1024]{0:T(1024)S(1)} %pad_clamp_fusion), kind=kCustom, calls=%fused_computation | custom fusion | bytes 4194368 | tf_op jit(solution)/shard_map/jit(_take)/gather | solution.py:149
  16.7 2.9 %fusion.50 = (f32[1024,128]{1,0:T(8,128)}, f32[1024,128]{1,0:T(8,128)}) fusion(f32[1024,64]{1,0:T(8,128)S(1)} %broadcast_multiply_fusion), kind=kLoop, calls=%fused_computation.76 | loop fusion | flops 131072 | bytes 1310720 | tf_op jit(solution)/shard_map/cos | solution.py:31
  19.9 1.5 fusion.61
  21.3 25.2 %all-gather.3.cloned.1.call-done = bf16[1024,2048]{1,0:T(8,128)(2,1)} async-done(((bf16[128,2048]{1,0:T(8,128)(2,1)}), bf16[1024,2048]{1,0:T(8,128)(2,1)}) %all-gather.3.cloned.1.call-update) | async-done | bytes 4194320 | tf_op jit(solution)/shard_map/all_gather | solution.py:133
  46.6 5.2 %add_bitcast_fusion = f32[3,1024,256]{2,1,0:T(8,128)S(1)} fusion(bf16[3,2048,256]{2,1,0:T(8,128)(2,1)S(1)} %copy-done, bf16[1024,2048]{1,0:T(8,128)(2,1)} %all-gather.3.cloned.1.call-done, f32[3,256]{1,0:T(4,128)S(1)} %convert_element_type.106), kind=kOutput, calls=%fused_computation.15 | convolution fusion | flops 3222011904 | bytes 10488832 | tf_op jit(solution)/shard_map/td,cdf->ctf/dot_general | solution.py:137
  54.6 2.3 slice_negate_fusion
  57.0 2.3 maximum_multiply_fusion.1
  59.7 1.2 fusion.42
  60.9 1.3 pad_maximum_fusion.key_ref
  62.9 1.3 pad_maximum_fusion.1.value_ref
  64.1 16.6 %shard_map.154 = bf16[1024,256]{1,0:T(8,128)(2,1)} custom-call(s32[1]{0:T(128)} %copy.71.context_ref, bf16[1024,256]{1,0:T(8,128)(2,1)} %get-tuple-element.6.query_ref, bf16[3072,256]{1,0:T(8,128)(2,1)} %pad_maximum_fusion.key_ref, bf16[3072,256]{1,0:T(8,128)(2,1)} %pad_maximum_fusion.1.value_ref), custom_call_target="tpu_custom_call" | custom-call | tf_op jit(solution)/shard_map/pallas_call | solution.py:86
  80.7 4.3 %convolution_convert_fusion.1 = bf16[1024,2048]{1,0:T(8,128)(2,1)} fusion(bf16[1024,256]{1,0:T(8,128)(2,1)} %shard_map.154, bf16[256,2048]{1,0:T(8,128)(2,1)S(1)} %copy-done.11), kind=kOutput, calls=%fused_computation.11 | convolution fusion | flops 1075838976 | bytes 5767168 | tf_op jit(solution)/shard_map/dot_general | solution.py:158
  85.6 34.1 %reduce-scatter.3.cloned.1.call-done = bf16[128,2048]{1,0:T(8,128)(2,1)} async-done(((bf16[1024,2048]{1,0:T(8,128)(2,1)}), bf16[128,2048]{1,0:T(8,128)(2,1)}) %reduce-scatter.3.cloned.1.call-update) | async-done | bytes 524304 | tf_op jit(solution)/shard_map/reduce_scatter | solution.py:157
  119.7 1.3 fusion.39
  121.0 2.0 fusion.41
  123.5 1.2 reduce-window.6
  125.5 1.9 fusion.26
  128.1 60.1 %all_to_all.10 = bf16[64,10,16,128]{3,2,1,0:T(8,128)(2,1)S(1)} all-to-all(bf16[64,10,16,128]{3,2,1,0:T(8,128)(2,1)S(1)} %bitcast.134), channel_id=1, replica_groups=mesh['tok'=16,'x'=4,'core'=2] {'tok','x'}, dimensions={0} | all-to-all | bytes 5242880 | tf_op jit(solution)/shard_map/all_to_all | solution.py:196
  188.3 2.2 copy.70
  191.5 9.6 %fusion.4 = f32[1024,2,704]{0,2,1:T(8,128)S(1)} fusion(bf16[2048,2,704]{0,2,1:T(8,128)(2,1)} %param.29, bf16[1024,2048]{1,0:T(8,128)(2,1)} %all-gather.5.cloned.1.call-done), kind=kOutput, calls=%fused_computation.6 | convolution fusion | flops 5905580032 | bytes 15728640 | tf_op jit(solution)/shard_map/td,dcf->tcf/dot_general | solution.py:165
  201.1 5.3 %convolution_convert_fusion = bf16[1024,2048]{1,0:T(8,128)(2,1)} fusion(bf16[704,2048]{1,0:T(8,128)(2,1)S(1)} %copy-done.16, f32[1024,2,704]{0,2,1:T(8,128)S(1)} %fusion.4), kind=kOutput, calls=%fused_computation.10 | convolution fusion | flops 2959212544 | bytes 12845056 | tf_op jit(solution)/shard_map/dot_general | solution.py:172
  206.4 7.5 %fusion = f32[640,1408]{1,0:T(8,128)S(1)} fusion(bf16[640,2048]{1,0:T(8,128)(2,1)} %collective-permute-done, bf16[1,2048,1408]{2,1,0:T(8,128)(2,1)} %param.27), kind=kOutput, calls=%fused_computation.1 | convolution fusion | flops 3690987520 | bytes 11993088 | tf_op jit(solution)/shard_map/dot_general | solution.py:202
  214.0 2.3 convolution_convert_fusion.2
  216.6 6.7 %fusion.2 = f32[640,1408]{1,0:T(8,128)S(1)} fusion(bf16[1,2048,1408]{2,1,0:T(8,128)(2,1)} %param.27, bf16[80,8,16,128]{3,2,1,0:T(8,128)(2,1)S(1)} %bitcast.133), kind=kOutput, calls=%fused_computation.3 | convolution fusion | flops 3690987520 | bytes 11993088 | tf_op jit(solution)/shard_map/dot_general | solution.py:202
  223.3 2.4 fusion.12
  225.7 2.4 copy.53
  228.1 5.7 %all-to-all-start.1 = ((bf16[64,10,16,128]{3,2,1,0:T(8,128)(2,1)}), bf16[64,10,16,128]{3,2,1,0:T(8,128)(2,1)}, u32[]{:S(2)}, u32[]{:S(2)}) async-start(bf16[64,10,16,128]{3,2,1,0:T(8,128)(2,1)} %bitcast.35), calls=%async_computation.3 | async-start | bytes 5242880 | tf_op jit(solution)/shard_map/all_to_all | solution.py:214
  234.0 1.4 fusion.34
  235.5 36.0 %all-to-all-done.1 = bf16[64,10,16,128]{3,2,1,0:T(8,128)(2,1)} async-done(((bf16[64,10,16,128]{3,2,1,0:T(8,128)(2,1)}), bf16[64,10,16,128]{3,2,1,0:T(8,128)(2,1)}, u32[]{:S(2)}, u32[]{:S(2)}) %all-to-all-start.1) | async-done | bytes 2621472 | tf_op jit(solution)/shard_map/all_to_all | solution.py:214
  271.5 4.5 %fusion.21 = bf16[128,2048]{1,0:T(8,128)(2,1)} fusion(f32[128,640]{1,0:T(8,128)S(1)} %select_reduce_fusion, bf16[80,8,16,128]{3,2,1,0:T(8,128)(2,1)} %bitcast.37, bf16[128,2048]{1,0:T(8,128)(2,1)} %reduce-scatter.5.cloned.1.call-done, f32[128]{0:T(128)S(1)} %fusion.34, bf16[128,2048]{1,0:T(8,128)(2,1)} %reduce-scatter.3.cloned.1.call-done, ...), kind=kOutput, calls=%fused_computation.28 | convolution fusion | flops 2015887360 | bytes 5046784 | tf_op jit(solution)/shard_map/dot_general | solution.py:226
  (84 shorter events, 10.9 us)
Async XLA Ops:
  6.5 40.0 %copy-start = (bf16[3,2048,256]{2,1,0:T(8,128)(2,1)S(1)}, bf16[3,2048,256]{2,1,0:T(8,128)(2,1)}, u32[]{:S(2)}) copy-start(bf16[3,2048,256]{2,1,0:T(8,128)(2,1)} %param.21) | copy-start | bytes 9437188
  6.5 40.0 %all-gather.3.cloned.1.call-start = ((), (), s32[]{:S(2)}) async-start(), calls=%async_computation.4 | async-start | bytes 4718592 | tf_op jit(solution)/shard_map/all_gather | solution.py:133
  10.8 108.9 %reduce-scatter.3.cloned.1.call-start = ((), (), s32[]{:S(2)}) async-start(), calls=%async_computation.5 | async-start | bytes 4718592 | tf_op jit(solution)/shard_map/reduce_scatter | solution.py:157
  12.8 6.7 %copy-start.18 = (s32[1,16]{1,0:T(1,128)S(1)}, s32[1,16]{1,0:T(1,128)}, u32[]{:S(2)}) copy-start(s32[1,16]{1,0:T(1,128)} %param.18) | copy-start | bytes 196
  16.5 3.1 %copy-start.2 = (bf16[16,2,128,256]{3,2,1,0:T(8,128)(2,1)S(1)}, bf16[16,2,128,256]{3,2,1,0:T(8,128)(2,1)}, u32[]{:S(2)}) copy-start(bf16[16,2,128,256]{3,2,1,0:T(8,128)(2,1)} %gather_fusion) | copy-start | bytes 6291460
  51.8 1.8 copy-start.4
  54.6 2.3 copy-start.10
  57.0 2.4 copy-start.8
  57.0 2.7 copy-start.5
  59.7 1.2 copy-start.7
  60.9 1.7 copy-start.6
  60.9 1.9 copy-start.9
  64.1 16.6 %copy-start.11 = (bf16[256,2048]{1,0:T(8,128)(2,1)S(1)}, bf16[256,2048]{1,0:T(8,128)(2,1)}, u32[]{:S(2)}) copy-start(bf16[256,2048]{1,0:T(8,128)(2,1)} %param.23) | copy-start | bytes 3145732
  84.9 0.7 copy-start.13
  84.9 34.8 %copy-start.3 = (bf16[128,2048]{1,0:T(8,128)(2,1)S(1)}, bf16[128,2048]{1,0:T(8,128)(2,1)}, u32[]{:S(2)}) copy-start(bf16[128,2048]{1,0:T(8,128)(2,1)} %param.16) | copy-start | bytes 1572868
  84.9 38.2 %copy-start.12 = (s32[128,4]{0,1:T(4,128)S(1)}, s32[128,4]{0,1:T(4,128)}, u32[]{:S(2)}) copy-start(s32[128,4]{0,1:T(4,128)} %param.25) | copy-start | bytes 6148
  85.0 106.5 %all-gather.5.cloned.1.call-start = ((), (), s32[]{:S(2)}) async-start(), calls=%async_computation.6 | async-start | bytes 4718592 | tf_op jit(solution)/shard_map/all_gather | solution.py:167
  123.1 148.4 %reduce-scatter.5.cloned.1.call-start = ((), (), s32[]{:S(2)}) async-start(), calls=%async_computation.7 | async-start | bytes 4718592 | tf_op jit(solution)/shard_map/reduce_scatter | solution.py:173
  190.5 15.9 %collective-permute-start = (bf16[640,2048]{1,0:T(8,128)(2,1)}, bf16[640,2048]{1,0:T(8,128)(2,1)}, u32[]{:S(2)}, u32[]{:S(2)}) collective-permute-start(bf16[640,2048]{1,0:T(8,128)(2,1)} %bitcast.130), channel_id=1, source_target_pairs={{0,1},{1,0},{2,3},{3,2},{4,5},{5,4},{6,7},{7,6},{8,9},{9,8},{10,11... | collective-permute-start | bytes 7864328 | tf_op jit(solution)/shard_map/ppermute | solution.py:199
  191.5 9.6 %copy-start.16 = (bf16[704,2048]{1,0:T(8,128)(2,1)S(1)}, bf16[704,2048]{1,0:T(8,128)(2,1)}, u32[]{:S(2)}) copy-start(bf16[704,2048]{1,0:T(8,128)(2,1)} %param.30) | copy-start | bytes 8650756
  206.4 7.6 %copy-start.17 = (bf16[1,704,2048]{2,1,0:T(8,128)(2,1)S(1)}, bf16[1,704,2048]{2,1,0:T(8,128)(2,1)}, u32[]{:S(2)}) copy-start(bf16[1,704,2048]{2,1,0:T(8,128)(2,1)} %param.28) | copy-start | bytes 8650756
  216.3 7.0 %collective-permute-start.1 = (bf16[640,2048]{1,0:T(8,128)(2,1)S(1)}, bf16[640,2048]{1,0:T(8,128)(2,1)S(1)}, u32[]{:S(2)}, u32[]{:S(2)}) collective-permute-start(bf16[640,2048]{1,0:T(8,128)(2,1)S(1)} %convolution_convert_fusion.2), channel_id=1, source_target_pairs={{0,1},{1,0},{2,3},{3,2},{4,5},{5,4},{6,7},{7,6},{8,9},{9,8},{10,11... | collective-permute-start | bytes 7864328 | tf_op jit(solution)/shard_map/ppermute | solution.py:210
  228.1 5.7 %copy-start.14 = (bf16[2048]{0:T(1024)(128)(2,1)S(1)}, bf16[2048]{0:T(1024)(128)(2,1)}, u32[]{:S(2)}) copy-start(bf16[2048]{0:T(1024)(128)(2,1)} %param.31) | copy-start | bytes 12292
  228.1 5.7 %copy-start.15 = (f32[128,4]{0,1:T(4,128)S(1)}, f32[128,4]{0,1:T(4,128)}, u32[]{:S(2)}) copy-start(f32[128,4]{0,1:T(4,128)} %param.26) | copy-start | bytes 6148
  228.1 43.4 %all-to-all-start.1 = ((bf16[64,10,16,128]{3,2,1,0:T(8,128)(2,1)}), bf16[64,10,16,128]{3,2,1,0:T(8,128)(2,1)}, u32[]{:S(2)}, u32[]{:S(2)}) async-start(bf16[64,10,16,128]{3,2,1,0:T(8,128)(2,1)} %bitcast.35), calls=%async_computation.3 | async-start | bytes 5242880 | tf_op jit(solution)/shard_map/all_to_all | solution.py:214
  233.8 42.1 %copy-start.1 = (bf16[3,2048,256]{2,1,0:T(8,128)(2,1)S(1)}, bf16[3,2048,256]{2,1,0:T(8,128)(2,1)}, u32[]{:S(2)}) copy-start(bf16[3,2048,256]{2,1,0:T(8,128)(2,1)} %param.21) | copy-start | bytes 9437188
Sparse Core Ops, SparseCore 0:
  10.9 35.6 all-gather.2
  85.1 34.5 reduce-scatter.2
  123.2 60.5 all-gather.4
  206.5 30.3 reduce-scatter.4

commit v8 on v7

--- a/solution.py
+++ b/solution.py
@@ -42,17 +42,11 @@
     def kernel(context_ref, query_ref, key_ref, value_ref, out_ref):
         query = query_ref[...]
         dims = (((1,), (1,)), ((), ()))
-        cached_scores = (
-            lax.dot_general(
-                query, key_ref[:span_len, :], dims, preferred_element_type=jnp.float32
-            )
-            * scale
-        )
-        new_scores = (
-            lax.dot_general(
-                query, key_ref[span_len:, :], dims, preferred_element_type=jnp.float32
-            )
-            * scale
+        cached_scores = lax.dot_general(
+            query, key_ref[:span_len, :], dims, preferred_element_type=jnp.float32
+        )
+        new_scores = lax.dot_general(
+            query, key_ref[span_len:, :], dims, preferred_element_type=jnp.float32
         )
         cached_pos = lax.broadcasted_iota(jnp.int32, cached_scores.shape, 1)
         cached_scores = jnp.where(cached_pos < context_ref[0], cached_scores, -1e30)
@@ -65,8 +59,8 @@
             jnp.max(cached_scores, axis=-1, keepdims=True),
             jnp.max(new_scores, axis=-1, keepdims=True),
         )
-        cached_weights = jnp.exp(cached_scores - largest)
-        new_weights = jnp.exp(new_scores - largest)
+        cached_weights = jnp.exp((cached_scores - largest) * scale)
+        new_weights = jnp.exp((new_scores - largest) * scale)
         total = 1.0 / (
             jnp.sum(cached_weights, axis=-1, keepdims=True)
             + jnp.sum(new_weights, axis=-1, keepdims=True)

time: 283 us -> 284 us (level)
  no operation moved by 1% of the time
where the time goes in v8:
time: 284 us; the launch traced here: 283 us
  waiting for transfers between devices  95.4 us (34%)
  blocking collectives  60 us (21%)
  matrix products  51 us (18%)
  other arithmetic  22.4 us (8%)
  Pallas kernels  17.3 us (6%)
  local copies, waits for them, and re-layouts  15.6 us (5%)
  between operations  14.1 us (5%)
  starting transfers between devices  7.3 us (3%)
    all_to_all x1, blocking collectives, per_device(): lax.all_to_all(buffer.reshape(tiles), ('tok', 'x'), 0, 0, tiled=True)  60 us
    all_to_all x1, waiting for transfers between devices, per_device(): lax.all_to_all(merged_own.reshape(tiles), ('tok', 'x'), 0, 0, tiled=True)  36 us
    reduce_scatter x1, waiting for transfers between devices, per_device(): lax.psum_scatter(jnp.dot(heads_out, out_weight, preferred_element_type=jn...  34.1 us
    all_gather x1, waiting for transfers between devices, per_device(): lax.all_gather(rms_scale(hidden_in, attn_gain), HEAD, axis=0, tiled=True)  25.2 us
    pallas_call x1, Pallas kernels, attend(): pl.pallas_call(kernel, out_shape=jax.ShapeDtypeStruct((row_count, width),...  17.3 us
    dot_general x2, matrix products, half_expert(): inner = jnp.dot(rows, w_experts_in[0], preferred_element_type=jnp.float32)  14.2 us
    dot_general x1, matrix products, per_device(): jnp.einsum('td,dcf->tcf', lax.all_gather(mixed, HEAD, axis=0, tiled=True)...  9.58 us
    unnamed x43, local copies, waits for them, and re-layouts  7.29 us
  transfers between devices with their start and end apart: 7, of which 3 were waited for; matrix products, arithmetic and copies ran while one was open for 19% of the time, Pallas kernels for 0%

profile of v8, /device:TPU:1, one launch (start us, length us, event | category | flops | bytes accessed | tf_op | source)
XLA Modules:
  0.0 283.1 jit_solution(14134025499384496400)
XLA Ops:
  7.4 1.3 fusion.35
  8.7 2.0 fusion.37
  12.8 3.6 %gather_fusion = bf16[16,2,128,256]{3,2,1,0:T(8,128)(2,1)} fusion(bf16[2,16,128,256]{3,2,1,0:T(8,128)(2,1)} %param.19, s32[1024]{0:T(1024)S(1)} %pad_clamp_fusion), kind=kCustom, calls=%fused_computation | custom fusion | bytes 4194368 | tf_op jit(solution)/shard_map/jit(_take)/gather | solution.py:143
  16.7 2.9 %fusion.50 = (f32[1024,128]{1,0:T(8,128)}, f32[1024,128]{1,0:T(8,128)}) fusion(f32[1024,64]{1,0:T(8,128)S(1)} %broadcast_multiply_fusion), kind=kLoop, calls=%fused_computation.76 | loop fusion | flops 131072 | bytes 1310720 | tf_op jit(solution)/shard_map/cos | solution.py:31
  19.9 1.5 fusion.61
  21.3 25.2 %all-gather.3.cloned.1.call-done = bf16[1024,2048]{1,0:T(8,128)(2,1)} async-done(((bf16[128,2048]{1,0:T(8,128)(2,1)}), bf16[1024,2048]{1,0:T(8,128)(2,1)}) %all-gather.3.cloned.1.call-update) | async-done | bytes 4194320 | tf_op jit(solution)/shard_map/all_gather | solution.py:127
  46.6 5.2 %add_bitcast_fusion = f32[3,1024,256]{2,1,0:T(8,128)S(1)} fusion(bf16[3,2048,256]{2,1,0:T(8,128)(2,1)S(1)} %copy-done, bf16[1024,2048]{1,0:T(8,128)(2,1)} %all-gather.3.cloned.1.call-done, f32[3,256]{1,0:T(4,128)S(1)} %convert_element_type.106), kind=kOutput, calls=%fused_computation.15 | convolution fusion | flops 3222011904 | bytes 10488832 | tf_op jit(solution)/shard_map/td,cdf->ctf/dot_general | solution.py:131
  54.6 2.3 slice_negate_fusion
  57.0 2.3 maximum_multiply_fusion.1
  59.7 1.2 fusion.42
  60.9 1.3 pad_maximum_fusion.key_ref
  62.9 1.3 pad_maximum_fusion.1.value_ref
  64.1 17.3 %shard_map.154 = bf16[1024,256]{1,0:T(8,128)(2,1)} custom-call(s32[1]{0:T(128)} %copy.71.context_ref, bf16[1024,256]{1,0:T(8,128)(2,1)} %get-tuple-element.6.query_ref, bf16[3072,256]{1,0:T(8,128)(2,1)} %pad_maximum_fusion.key_ref, bf16[3072,256]{1,0:T(8,128)(2,1)} %pad_maximum_fusion.1.value_ref), custom_call_target="tpu_custom_call" | custom-call | tf_op jit(solution)/shard_map/pallas_call | solution.py:80
  81.4 4.3 %convolution_convert_fusion.1 = bf16[1024,2048]{1,0:T(8,128)(2,1)} fusion(bf16[1024,256]{1,0:T(8,128)(2,1)} %shard_map.154, bf16[256,2048]{1,0:T(8,128)(2,1)S(1)} %copy-done.11), kind=kOutput, calls=%fused_computation.11 | convolution fusion | flops 1075838976 | bytes 5767168 | tf_op jit(solution)/shard_map/dot_general | solution.py:152
  86.4 34.1 %reduce-scatter.3.cloned.1.call-done = bf16[128,2048]{1,0:T(8,128)(2,1)} async-done(((bf16[1024,2048]{1,0:T(8,128)(2,1)}), bf16[128,2048]{1,0:T(8,128)(2,1)}) %reduce-scatter.3.cloned.1.call-update) | async-done | bytes 524304 | tf_op jit(solution)/shard_map/reduce_scatter | solution.py:151
  120.5 1.3 fusion.39
  121.8 2.0 fusion.41
  124.2 1.2 reduce-window.6
  126.2 1.9 fusion.26
  128.9 60.0 %all_to_all.10 = bf16[64,10,16,128]{3,2,1,0:T(8,128)(2,1)S(1)} all-to-all(bf16[64,10,16,128]{3,2,1,0:T(8,128)(2,1)S(1)} %bitcast.134), channel_id=1, replica_groups=mesh['tok'=16,'x'=4,'core'=2] {'tok','x'}, dimensions={0} | all-to-all | bytes 5242880 | tf_op jit(solution)/shard_map/all_to_all | solution.py:190
  188.9 2.2 copy.70
  192.1 9.6 %fusion.4 = f32[1024,2,704]{0,2,1:T(8,128)S(1)} fusion(bf16[2048,2,704]{0,2,1:T(8,128)(2,1)} %param.29, bf16[1024,2048]{1,0:T(8,128)(2,1)} %all-gather.5.cloned.1.call-done), kind=kOutput, calls=%fused_computation.6 | convolution fusion | flops 5905580032 | bytes 15728640 | tf_op jit(solution)/shard_map/td,dcf->tcf/dot_general | solution.py:159
  201.7 5.3 %convolution_convert_fusion = bf16[1024,2048]{1,0:T(8,128)(2,1)} fusion(bf16[704,2048]{1,0:T(8,128)(2,1)S(1)} %copy-done.16, f32[1024,2,704]{0,2,1:T(8,128)S(1)} %fusion.4), kind=kOutput, calls=%fused_computation.10 | convolution fusion | flops 2959212544 | bytes 12845056 | tf_op jit(solution)/shard_map/dot_general | solution.py:166
  207.1 7.5 %fusion = f32[640,1408]{1,0:T(8,128)S(1)} fusion(bf16[640,2048]{1,0:T(8,128)(2,1)} %collective-permute-done, bf16[1,2048,1408]{2,1,0:T(8,128)(2,1)} %param.27), kind=kOutput, calls=%fused_computation.1 | convolution fusion | flops 3690987520 | bytes 11993088 | tf_op jit(solution)/shard_map/dot_general | solution.py:196
  214.6 2.3 convolution_convert_fusion.2
  217.2 6.7 %fusion.2 = f32[640,1408]{1,0:T(8,128)S(1)} fusion(bf16[1,2048,1408]{2,1,0:T(8,128)(2,1)} %param.27, bf16[80,8,16,128]{3,2,1,0:T(8,128)(2,1)S(1)} %bitcast.133), kind=kOutput, calls=%fused_computation.3 | convolution fusion | flops 3690987520 | bytes 11993088 | tf_op jit(solution)/shard_map/dot_general | solution.py:196
  223.9 2.4 fusion.12
  226.3 2.4 copy.53
  228.7 5.7 %all-to-all-start.1 = ((bf16[64,10,16,128]{3,2,1,0:T(8,128)(2,1)}), bf16[64,10,16,128]{3,2,1,0:T(8,128)(2,1)}, u32[]{:S(2)}, u32[]{:S(2)}) async-start(bf16[64,10,16,128]{3,2,1,0:T(8,128)(2,1)} %bitcast.35), calls=%async_computation.3 | async-start | bytes 5242880 | tf_op jit(solution)/shard_map/all_to_all | solution.py:208
  234.7 1.4 fusion.34
  236.1 36.0 %all-to-all-done.1 = bf16[64,10,16,128]{3,2,1,0:T(8,128)(2,1)} async-done(((bf16[64,10,16,128]{3,2,1,0:T(8,128)(2,1)}), bf16[64,10,16,128]{3,2,1,0:T(8,128)(2,1)}, u32[]{:S(2)}, u32[]{:S(2)}) %all-to-all-start.1) | async-done | bytes 2621472 | tf_op jit(solution)/shard_map/all_to_all | solution.py:208
  272.2 4.5 %fusion.21 = bf16[128,2048]{1,0:T(8,128)(2,1)} fusion(f32[128,640]{1,0:T(8,128)S(1)} %select_reduce_fusion, bf16[80,8,16,128]{3,2,1,0:T(8,128)(2,1)} %bitcast.37, bf16[128,2048]{1,0:T(8,128)(2,1)} %reduce-scatter.5.cloned.1.call-done, f32[128]{0:T(128)S(1)} %fusion.34, bf16[128,2048]{1,0:T(8,128)(2,1)} %reduce-scatter.3.cloned.1.call-done, ...), kind=kOutput, calls=%fused_computation.28 | convolution fusion | flops 2015887360 | bytes 5046784 | tf_op jit(solution)/shard_map/dot_general | solution.py:220
  (84 shorter events, 10.9 us)
Async XLA Ops:
  6.5 40.0 %copy-start = (bf16[3,2048,256]{2,1,0:T(8,128)(2,1)S(1)}, bf16[3,2048,256]{2,1,0:T(8,128)(2,1)}, u32[]{:S(2)}) copy-start(bf16[3,2048,256]{2,1,0:T(8,128)(2,1)} %param.21) | copy-start | bytes 9437188
  6.5 40.0 %all-gather.3.cloned.1.call-start = ((), (), s32[]{:S(2)}) async-start(), calls=%async_computation.4 | async-start | bytes 4718592 | tf_op jit(solution)/shard_map/all_gather | solution.py:127
  10.8 109.7 %reduce-scatter.3.cloned.1.call-start = ((), (), s32[]{:S(2)}) async-start(), calls=%async_computation.5 | async-start | bytes 4718592 | tf_op jit(solution)/shard_map/reduce_scatter | solution.py:151
  12.8 6.7 %copy-start.18 = (s32[1,16]{1,0:T(1,128)S(1)}, s32[1,16]{1,0:T(1,128)}, u32[]{:S(2)}) copy-start(s32[1,16]{1,0:T(1,128)} %param.18) | copy-start | bytes 196
  16.5 3.1 %copy-start.2 = (bf16[16,2,128,256]{3,2,1,0:T(8,128)(2,1)S(1)}, bf16[16,2,128,256]{3,2,1,0:T(8,128)(2,1)}, u32[]{:S(2)}) copy-start(bf16[16,2,128,256]{3,2,1,0:T(8,128)(2,1)} %gather_fusion) | copy-start | bytes 6291460
  51.8 1.8 copy-start.4
  54.6 2.3 copy-start.10
  57.0 2.4 copy-start.8
  57.0 2.7 copy-start.5
  59.7 1.2 copy-start.7
  60.9 1.7 copy-start.6
  60.9 1.9 copy-start.9
  64.1 17.3 %copy-start.11 = (bf16[256,2048]{1,0:T(8,128)(2,1)S(1)}, bf16[256,2048]{1,0:T(8,128)(2,1)}, u32[]{:S(2)}) copy-start(bf16[256,2048]{1,0:T(8,128)(2,1)} %param.23) | copy-start | bytes 3145732
  85.7 0.7 copy-start.13
  85.7 34.8 %copy-start.3 = (bf16[128,2048]{1,0:T(8,128)(2,1)S(1)}, bf16[128,2048]{1,0:T(8,128)(2,1)}, u32[]{:S(2)}) copy-start(bf16[128,2048]{1,0:T(8,128)(2,1)} %param.16) | copy-start | bytes 1572868
  85.7 38.2 %copy-start.12 = (s32[128,4]{0,1:T(4,128)S(1)}, s32[128,4]{0,1:T(4,128)}, u32[]{:S(2)}) copy-start(s32[128,4]{0,1:T(4,128)} %param.25) | copy-start | bytes 6148
  85.7 106.4 %all-gather.5.cloned.1.call-start = ((), (), s32[]{:S(2)}) async-start(), calls=%async_computation.6 | async-start | bytes 4718592 | tf_op jit(solution)/shard_map/all_gather | solution.py:161
  123.8 148.3 %reduce-scatter.5.cloned.1.call-start = ((), (), s32[]{:S(2)}) async-start(), calls=%async_computation.7 | async-start | bytes 4718592 | tf_op jit(solution)/shard_map/reduce_scatter | solution.py:167
  191.1 15.9 %collective-permute-start = (bf16[640,2048]{1,0:T(8,128)(2,1)}, bf16[640,2048]{1,0:T(8,128)(2,1)}, u32[]{:S(2)}, u32[]{:S(2)}) collective-permute-start(bf16[640,2048]{1,0:T(8,128)(2,1)} %bitcast.130), channel_id=1, source_target_pairs={{0,1},{1,0},{2,3},{3,2},{4,5},{5,4},{6,7},{7,6},{8,9},{9,8},{10,11... | collective-permute-start | bytes 7864328 | tf_op jit(solution)/shard_map/ppermute | solution.py:193
  192.1 9.6 %copy-start.16 = (bf16[704,2048]{1,0:T(8,128)(2,1)S(1)}, bf16[704,2048]{1,0:T(8,128)(2,1)}, u32[]{:S(2)}) copy-start(bf16[704,2048]{1,0:T(8,128)(2,1)} %param.30) | copy-start | bytes 8650756
  207.0 7.6 %copy-start.17 = (bf16[1,704,2048]{2,1,0:T(8,128)(2,1)S(1)}, bf16[1,704,2048]{2,1,0:T(8,128)(2,1)}, u32[]{:S(2)}) copy-start(bf16[1,704,2048]{2,1,0:T(8,128)(2,1)} %param.28) | copy-start | bytes 8650756
  216.9 7.0 %collective-permute-start.1 = (bf16[640,2048]{1,0:T(8,128)(2,1)S(1)}, bf16[640,2048]{1,0:T(8,128)(2,1)S(1)}, u32[]{:S(2)}, u32[]{:S(2)}) collective-permute-start(bf16[640,2048]{1,0:T(8,128)(2,1)S(1)} %convolution_convert_fusion.2), channel_id=1, source_target_pairs={{0,1},{1,0},{2,3},{3,2},{4,5},{5,4},{6,7},{7,6},{8,9},{9,8},{10,11... | collective-permute-start | bytes 7864328 | tf_op jit(solution)/shard_map/ppermute | solution.py:204
  228.7 5.7 %copy-start.14 = (bf16[2048]{0:T(1024)(128)(2,1)S(1)}, bf16[2048]{0:T(1024)(128)(2,1)}, u32[]{:S(2)}) copy-start(bf16[2048]{0:T(1024)(128)(2,1)} %param.31) | copy-start | bytes 12292
  228.7 5.7 %copy-start.15 = (f32[128,4]{0,1:T(4,128)S(1)}, f32[128,4]{0,1:T(4,128)}, u32[]{:S(2)}) copy-start(f32[128,4]{0,1:T(4,128)} %param.26) | copy-start | bytes 6148
  228.7 43.4 %all-to-all-start.1 = ((bf16[64,10,16,128]{3,2,1,0:T(8,128)(2,1)}), bf16[64,10,16,128]{3,2,1,0:T(8,128)(2,1)}, u32[]{:S(2)}, u32[]{:S(2)}) async-start(bf16[64,10,16,128]{3,2,1,0:T(8,128)(2,1)} %bitcast.35), calls=%async_computation.3 | async-start | bytes 5242880 | tf_op jit(solution)/shard_map/all_to_all | solution.py:208
  234.5 42.1 %copy-start.1 = (bf16[3,2048,256]{2,1,0:T(8,128)(2,1)S(1)}, bf16[3,2048,256]{2,1,0:T(8,128)(2,1)}, u32[]{:S(2)}) copy-start(bf16[3,2048,256]{2,1,0:T(8,128)(2,1)} %param.21) | copy-start | bytes 9437188
Sparse Core Ops, SparseCore 0:
  10.9 35.6 all-gather.2
  85.8 34.5 reduce-scatter.2
  123.9 60.4 all-gather.4
  207.2 30.3 reduce-scatter.4
